TPU v7x, 256 devices: a whole 4x4x8 slice. The times are simulated.
256 devices in a mesh: seq: 64 (over x, z, core), ch: 4 (over y).
Axes of the slice: x: 4, y: 4, z: 8, core: 2. Of those that a mesh axis runs over, the one named last changes fastest.
Arguments:
- inputs: bfloat16 [8192, 4096], P('seq'), may hold values from -6 to 6
- norm_gain: float32 [4096], replicated, may hold values from 0.1 to 1.9
- in_weight: bfloat16 [4096, 3, 1024], P('seq', None, 'ch'), may hold values from -0.09375 to 0.09375
- short_filter: float32 [3, 3, 1024], P(None, None, 'ch'), may hold values from -4 to 4
- long_filter: float32 [8192, 1024], P('seq', 'ch'), may hold values from -2.2 to 2.2
- conv_bias: float32 [1024], P('ch'), may hold values from -4 to 4
- out_weight: bfloat16 [1024, 4096], P('ch', 'seq'), may hold values from -0.1875 to 0.1875
- out_grad: bfloat16 [8192, 4096], P('seq'), may hold values from -6 to 6
Outputs:
- block_out: bfloat16 [8192, 4096], P('seq', 'ch')
- in_grad: bfloat16 [8192, 4096], P('seq')
- filter_grad: float32 [8192, 1024], P('seq', 'ch')
All inputs are finite; a program needn't handle non-finite values.
Results may differ from a plain program's by a relative error of at most 0.013.
Values may be sent and summed in bfloat16 or wider, within the bound.
No kernel may reach another device: no remote copies, remote signals or barrier semaphores. Data moves between devices by JAX's collectives and lax.ppermute only.
A program may use at most 64 MiB of HBM per device.

v0:
```python
import math

import jax
import jax.numpy as jnp
from jax import lax
from jax.sharding import PartitionSpec as P

epsilon = 1e-05
highest = lax.Precision.HIGHEST


def passed_along(block, axis, distance):
    devices = range(lax.axis_size(axis))
    route = [(i - distance, i) for i in devices if i - distance in devices]
    return lax.ppermute(block, axis, route)


def regroup(data):
    return lax.all_to_all(data, "seq", split_axis=2, concat_axis=1, tiled=True)


def device_table(devices):
    first = jnp.arange(2 * devices, dtype=jnp.int32)[:, None]
    second = jnp.arange(devices, dtype=jnp.int32)[None, :]
    turns = first * second % (2 * devices)
    phases = 2.0 * math.pi / (2 * devices) * turns.astype(jnp.float32)
    return (jnp.cos(phases), jnp.sin(phases))


def phase_table(devices, place, local_rows, sign):
    total_len = 2 * devices * local_rows
    halves = jnp.arange(2, dtype=jnp.int32)[:, None, None]
    upper = jnp.arange(local_rows, dtype=jnp.int32)[None, :, None]
    lower = jnp.arange(local_rows, dtype=jnp.int32)[None, None, :]
    freqs = 2 * place + halves + 2 * devices * upper
    turns = freqs * lower % total_len
    phases = sign * 2.0 * math.pi / total_len * turns.astype(jnp.float32)
    return (jnp.cos(phases), jnp.sin(phases))


def to_spectrum(signals):
    count = signals.shape[0]
    local_rows = signals.shape[1]
    slab_width = signals.shape[2]
    devices = lax.axis_size("seq")
    place = lax.axis_index("seq")
    share = local_rows // devices
    spread = regroup(signals.reshape(count, 1, local_rows, slab_width))
    cos_dev, sin_dev = device_table(devices)
    real_part = jnp.einsum("kb,ubtc->utkc", cos_dev, spread, precision=highest)
    imag_part = -jnp.einsum("kb,ubtc->utkc", sin_dev, spread, precision=highest)
    joined = jnp.stack([real_part, imag_part], 1).reshape(count * 2, share, 2 * devices, slab_width)
    arrived = regroup(joined).reshape(count, 2, local_rows, 2, slab_width)
    cos_loc, sin_loc = phase_table(devices, place, local_rows, -1.0)
    zero_real = arrived[:, 0]
    zero_imag = arrived[:, 1]
    spec_real = jnp.einsum("ekt,utec->ukec", cos_loc, zero_real, precision=highest) - jnp.einsum(
        "ekt,utec->ukec", sin_loc, zero_imag, precision=highest
    )
    spec_imag = jnp.einsum("ekt,utec->ukec", sin_loc, zero_real, precision=highest) + jnp.einsum(
        "ekt,utec->ukec", cos_loc, zero_imag, precision=highest
    )
    return (spec_real, spec_imag)


def to_signal(spec_real, spec_imag):
    count = spec_real.shape[0]
    local_rows = spec_real.shape[1]
    slab_width = spec_real.shape[3]
    devices = lax.axis_size("seq")
    place = lax.axis_index("seq")
    share = local_rows // devices
    cos_loc, sin_loc = phase_table(devices, place, local_rows, 1.0)
    back_real = jnp.einsum("ekt,ukec->uetc", cos_loc, spec_real, precision=highest) - jnp.einsum(
        "ekt,ukec->uetc", sin_loc, spec_imag, precision=highest
    )
    back_imag = jnp.einsum("ekt,ukec->uetc", sin_loc, spec_real, precision=highest) + jnp.einsum(
        "ekt,ukec->uetc", cos_loc, spec_imag, precision=highest
    )
    joined = jnp.stack([back_real, back_imag], 1).reshape(count * 2, 2, local_rows, slab_width)
    arrived = regroup(joined).reshape(count, 2, 2 * devices, share, slab_width)
    cos_dev, sin_dev = device_table(devices)
    signal = jnp.einsum("kb,uktc->utbc", cos_dev, arrived[:, 0], precision=highest) - jnp.einsum(
        "kb,uktc->utbc", sin_dev, arrived[:, 1], precision=highest
    )
    returned = regroup(signal)
    return returned.reshape(count, local_rows, slab_width) / float(2 * devices * local_rows)


def per_device(
    inputs, norm_gain, in_weight, short_filter, long_filter, conv_bias, out_weight, out_grad
):
    local_rows = inputs.shape[0]
    model_width = inputs.shape[1]
    slab_width = long_filter.shape[1]
    taps = short_filter.shape[1]
    wide_inputs = inputs.astype(jnp.float32)
    inv_rms = lax.rsqrt(jnp.mean(wide_inputs * wide_inputs, axis=1, keepdims=True) + epsilon)
    normed = (wide_inputs * inv_rms * norm_gain).astype(jnp.bfloat16)
    in_panel, out_panel = (
        lax.all_gather(in_weight, "seq", axis=0, tiled=True),
        lax.all_gather(out_weight, "seq", axis=1, tiled=True),
    )
    in_flat = in_panel.reshape(model_width, 3 * slab_width)
    projected = jnp.dot(normed, in_flat, preferred_element_type=jnp.float32)
    projected = projected.astype(jnp.bfloat16).reshape(local_rows, 3, slab_width)
    upper_rim = passed_along(projected[local_rows - (taps - 1) :], "seq", 1)
    extended = jnp.concatenate([upper_rim, projected], 0).astype(jnp.float32)
    mixed = jnp.zeros((local_rows, 3, slab_width), jnp.float32)
    for offset in range(taps):
        begin = taps - 1 - offset
        mixed = mixed + short_filter[:, offset, :][None] * extended[begin : begin + local_rows]
    query_br = mixed[:, 0]
    key_br = mixed[:, 1]
    value_br = mixed[:, 2]
    product = key_br * value_br
    spec_real, spec_imag = to_spectrum(jnp.stack([product, long_filter]))
    sig_real, filt_real = (spec_real[0], spec_real[1])
    sig_imag, filt_imag = (spec_imag[0], spec_imag[1])
    conv_real = sig_real * filt_real - sig_imag * filt_imag
    conv_imag = sig_real * filt_imag + sig_imag * filt_real
    conv_out = to_signal(conv_real[None], conv_imag[None])[0]
    biased = conv_out + conv_bias * product
    gated = (query_br * biased).astype(jnp.bfloat16)
    partial_out = jnp.dot(gated, out_panel, preferred_element_type=jnp.float32)
    summed = lax.psum_scatter(
        partial_out.astype(jnp.bfloat16), "ch", scatter_dimension=1, tiled=True
    ).astype(jnp.float32)
    share = summed.shape[1]
    residual = lax.dynamic_slice_in_dim(wide_inputs, lax.axis_index("ch") * share, share, 1)
    block_out = (residual + summed).astype(jnp.bfloat16)
    gate_grad = jnp.dot(out_grad, out_panel.T, preferred_element_type=jnp.float32)
    carried = gate_grad * query_br
    all_real, all_imag = to_spectrum(jnp.stack([product, long_filter, carried]))
    sig_real, filt_real, grad_real = (all_real[0], all_real[1], all_real[2])
    sig_imag, filt_imag, grad_imag = (all_imag[0], all_imag[1], all_imag[2])
    back_real = grad_real * filt_real + grad_imag * filt_imag
    back_imag = grad_imag * filt_real - grad_real * filt_imag
    pair_real = grad_real * sig_real + grad_imag * sig_imag
    pair_imag = grad_imag * sig_real - grad_real * sig_imag
    returned = to_signal(jnp.stack([back_real, pair_real]), jnp.stack([back_imag, pair_imag]))
    back_conv = returned[0]
    filter_grad = returned[1] * float(local_rows * lax.axis_size("seq")) ** (-0.5)
    source_grad = back_conv + conv_bias * carried
    mixed_grad = jnp.stack([gate_grad * biased, source_grad * value_br, source_grad * key_br], 1)
    lower_rim = passed_along(mixed_grad[: taps - 1], "seq", -1)
    extended_back = jnp.concatenate([mixed_grad, lower_rim], 0)
    proj_grad = jnp.zeros((local_rows, 3, slab_width), jnp.float32)
    for offset in range(taps):
        proj_grad = (
            proj_grad
            + short_filter[:, offset, :][None] * extended_back[offset : offset + local_rows]
        )
    proj_grad = proj_grad.astype(jnp.bfloat16).reshape(local_rows, 3 * slab_width)
    partial_grad = jnp.dot(proj_grad, in_flat.T, preferred_element_type=jnp.float32)
    norm_grad = lax.psum(partial_grad, "ch")
    weighted = norm_grad * norm_gain
    inner_term = jnp.mean(weighted * wide_inputs, axis=1, keepdims=True)
    in_grad = (
        out_grad.astype(jnp.float32) + weighted * inv_rms - wide_inputs * inv_rms**3 * inner_term
    ).astype(jnp.bfloat16)
    return (block_out, in_grad, filter_grad)


def solution(mesh):
    return jax.shard_map(
        per_device,
        mesh=mesh,
        in_specs=(
            P("seq", None),
            P(),
            P("seq", None, "ch"),
            P(None, None, "ch"),
            P("seq", "ch"),
            P("ch"),
            P("ch", "seq"),
            P("seq", None),
        ),
        out_specs=(P("seq", "ch"), P("seq", None), P("seq", "ch")),
        check_vma=False,
    )
```

profile of v0, /device:TPU:2, one launch (start us, length us, event | category | flops | bytes accessed | tf_op | source)
XLA Modules:
  0.0 497.1 jit_solution(17033071886096602538)
XLA Ops:
  11.6 81.5 %all-gather.3.cloned.1.call-done = bf16[4096,3,256]{2,0,1:T(8,128)(2,1)} async-done(((bf16[64,3,256]{2,0,1:T(8,128)(2,1)}), bf16[4096,3,256]{2,0,1:T(8,128)(2,1)}) %all-gather.3.cloned.1.call-update) | async-done | bytes 6291472 | tf_op jit(solution)/shard_map/all_gather | solution.py:101
  93.0 8.7 %copy.102 = bf16[4096,3,256]{0,2,1:T(8,128)(2,1)} copy(bf16[4096,3,256]{2,0,1:T(8,128)(2,1)} %all-gather.3.cloned.1.call-done) | data formatting | bytes 12582912 | tf_op jit(solution)/shard_map/all_gather | solution.py:101
  101.7 5.0 %convolution_convert_fusion.1 = bf16[128,768]{1,0:T(8,128)(2,1)S(1)} fusion(bf16[4096,768]{0,1:T(8,128)(2,1)} %bitcast.250, bf16[128,4096]{1,0:T(8,128)(2,1)S(1)} %copy-done, f32[4096]{0:T(1024)S(1)} %copy-done.13, f32[128]{0:T(128)S(1)} %get-tuple-element.27), kind=kOutput, calls=%fused_computation.25 | convolution fusion | flops 807501824 | bytes 7553536 | tf_op jit(solution)/shard_map/dot_general | solution.py:105
  109.4 4.5 collective-permute-done
  115.0 6.4 %all-to-all-start = ((f32[2,1,128,256]{3,0,1,2:T(2,128)}), f32[2,1,128,256]{3,0,1,2:T(2,128)S(1)}, u32[]{:S(2)}, u32[]{:S(2)}) async-start(f32[2,1,128,256]{3,0,1,2:T(2,128)} %copy.106), calls=%async_computation | async-start | bytes 524288 | tf_op jit(solution)/shard_map/all_to_all | solution.py:19
  121.4 49.0 %all-gather.5.cloned.1.call-done = bf16[256,4096]{0,1:T(8,128)(2,1)} async-done(((bf16[256,64]{0,1:T(8,128)(2,1)}), bf16[256,4096]{0,1:T(8,128)(2,1)}) %all-gather.5.cloned.1.call-update) | async-done | bytes 2097168 | tf_op jit(solution)/shard_map/all_gather | solution.py:102
  174.3 8.0 %all-to-all-start.4 = ((f32[3,1,128,256]{3,1,0,2:T(1,128)}), f32[3,1,128,256]{3,1,0,2:T(1,128)}, u32[]{:S(2)}, u32[]{:S(2)}) async-start(f32[3,1,128,256]{3,1,0,2:T(1,128)} %copy.118), calls=%async_computation.5 | async-start | bytes 786432 | tf_op jit(solution)/shard_map/all_to_all | solution.py:19
  186.6 9.7 %all-to-all-done.4 = f32[3,1,128,256]{3,1,0,2:T(1,128)} async-done(((f32[3,1,128,256]{3,1,0,2:T(1,128)}), f32[3,1,128,256]{3,1,0,2:T(1,128)}, u32[]{:S(2)}, u32[]{:S(2)}) %all-to-all-start.4) | async-done | bytes 393248 | tf_op jit(solution)/shard_map/all_to_all | solution.py:19
  196.3 20.6 %all-to-all-start.1 = ((f32[4,2,128,256]{3,1,0,2:T(2,128)}), f32[4,2,128,256]{3,1,0,2:T(2,128)}, u32[]{:S(2)}, u32[]{:S(2)}) async-start(f32[4,2,128,256]{3,1,0,2:T(2,128)} %copy.110), calls=%async_computation.1 | async-start | bytes 2097152 | tf_op jit(solution)/shard_map/all_to_all | solution.py:19
  222.8 3.8 copy.123
  226.6 16.9 %all-to-all-done.1 = f32[4,2,128,256]{3,1,0,2:T(2,128)} async-done(((f32[4,2,128,256]{3,1,0,2:T(2,128)}), f32[4,2,128,256]{3,1,0,2:T(2,128)}, u32[]{:S(2)}, u32[]{:S(2)}) %all-to-all-start.1) | async-done | bytes 1048608 | tf_op jit(solution)/shard_map/all_to_all | solution.py:19
  243.5 7.8 %all-to-all-start.5 = ((f32[6,2,128,256]{3,1,0,2:T(2,128)}), f32[6,2,128,256]{3,1,0,2:T(2,128)S(1)}, u32[]{:S(2)}, u32[]{:S(2)}) async-start(f32[6,2,128,256]{3,1,0,2:T(2,128)} %copy.123), calls=%async_computation.6 | async-start | bytes 3145728 | tf_op jit(solution)/shard_map/all_to_all | solution.py:19
  267.3 22.5 %all-to-all-done.5 = f32[6,2,128,256]{3,1,0,2:T(2,128)S(1)} async-done(((f32[6,2,128,256]{3,1,0,2:T(2,128)}), f32[6,2,128,256]{3,1,0,2:T(2,128)S(1)}, u32[]{:S(2)}, u32[]{:S(2)}) %all-to-all-start.5) | async-done | bytes 1572896 | tf_op jit(solution)/shard_map/all_to_all | solution.py:19
  289.8 7.6 %all-to-all-start.2 = ((f32[2,2,128,256]{3,1,0,2:T(2,128)}), f32[2,2,128,256]{3,1,0,2:T(2,128)}, u32[]{:S(2)}, u32[]{:S(2)}) async-start(f32[2,2,128,256]{3,1,0,2:T(2,128)} %copy.114), calls=%async_computation.2 | async-start | bytes 1048576 | tf_op jit(solution)/shard_map/all_to_all | solution.py:19
  317.2 10.3 %all-to-all-start.6 = ((f32[4,2,128,256]{3,1,0,2:T(2,128)}), f32[4,2,128,256]{3,1,0,2:T(2,128)S(1)}, u32[]{:S(2)}, u32[]{:S(2)}) async-start(f32[4,2,128,256]{3,1,0,2:T(2,128)} %copy.128), calls=%async_computation.7 | async-start | bytes 2097152 | tf_op jit(solution)/shard_map/all_to_all | solution.py:19
  330.7 23.7 %all-to-all-done.6 = f32[4,2,128,256]{3,1,0,2:T(2,128)S(1)} async-done(((f32[4,2,128,256]{3,1,0,2:T(2,128)}), f32[4,2,128,256]{3,1,0,2:T(2,128)S(1)}, u32[]{:S(2)}, u32[]{:S(2)}) %all-to-all-start.6) | async-done | bytes 1048608 | tf_op jit(solution)/shard_map/all_to_all | solution.py:19
  354.5 8.4 %all-to-all-start.3 = ((f32[1,2,64,256]{3,1,0,2:T(2,128)}), f32[1,2,64,256]{3,1,0,2:T(2,128)}, u32[]{:S(2)}, u32[]{:S(2)}) async-start(f32[1,2,64,256]{3,1,0,2:T(2,128)} %copy.117), calls=%async_computation.3 | async-start | bytes 262144 | tf_op jit(solution)/shard_map/all_to_all | solution.py:19
  365.8 6.1 %all-to-all-done.3 = f32[1,2,64,256]{3,1,0,2:T(2,128)} async-done(((f32[1,2,64,256]{3,1,0,2:T(2,128)}), f32[1,2,64,256]{3,1,0,2:T(2,128)}, u32[]{:S(2)}, u32[]{:S(2)}) %all-to-all-start.3) | async-done | bytes 131104 | tf_op jit(solution)/shard_map/all_to_all | solution.py:19
  371.9 6.1 %all-to-all-start.7 = ((f32[2,2,64,256]{3,1,0,2:T(2,128)}), f32[2,2,64,256]{3,1,0,2:T(2,128)}, u32[]{:S(2)}, u32[]{:S(2)}) async-start(f32[2,2,64,256]{3,1,0,2:T(2,128)} %copy.132), calls=%async_computation.8 | async-start | bytes 524288 | tf_op jit(solution)/shard_map/all_to_all | solution.py:19
  381.4 8.2 %all-to-all-done.7 = f32[2,2,64,256]{3,1,0,2:T(2,128)} async-done(((f32[2,2,64,256]{3,1,0,2:T(2,128)}), f32[2,2,64,256]{3,1,0,2:T(2,128)}, u32[]{:S(2)}, u32[]{:S(2)}) %all-to-all-start.7) | async-done | bytes 262176 | tf_op jit(solution)/shard_map/all_to_all | solution.py:19
  398.7 3.0 collective-permute-start.1
  403.0 6.5 %convolution_bitcast_fusion = f32[128,4096]{1,0:T(8,128)} fusion(bf16[4096,3,256]{2,0,1:T(8,128)(2,1)} %all-gather.3.cloned.1.call-done, f32[130,3,256]{2,0,1:T(8,128)S(1)} %pad_maximum_fusion.9, f32[3,256]{1,0:T(4,128)S(1)} %get-tuple-element.28, f32[3,256]{1,0:T(4,128)S(1)} %get-tuple-element.29, f32[3,256]{1,0:T(4,128)S(1)} %bitcast.267, ...), kind=kOutput, calls=%fused_computation | convolution fusion | flops 806092800 | bytes 9580544 | tf_op jit(solution)/shard_map/dot_general | solution.py:155
  411.9 8.5 %reduce-scatter.2.cloned.1.call-done = bf16[128,1024]{1,0:T(8,128)(2,1)} async-done(((bf16[128,4096]{1,0:T(8,128)(2,1)}), bf16[128,1024]{1,0:T(8,128)(2,1)}) %reduce-scatter.2.cloned.1.call-update) | async-done | bytes 262160 | tf_op jit(solution)/shard_map/reduce_scatter | solution.py:126
  422.3 63.9 %all-reduce.2.cloned.1.call-done = f32[128,4096]{1,0:T(8,128)} async-done(((f32[128,4096]{1,0:T(8,128)}), f32[128,4096]{1,0:T(8,128)}) %all-reduce.2.cloned.1.call-update) | async-done | bytes 2097168 | tf_op jit(solution)/shard_map/psum | solution.py:156
  (138 shorter events, 86.0 us)
Async XLA Ops:
  7.2 85.9 %all-gather.3.cloned.1.call-start = ((), (), s32[]{:S(2)}) async-start(), calls=%async_computation.9 | async-start | bytes 6389760 | tf_op jit(solution)/shard_map/all_gather | solution.py:101
  7.9 162.5 %all-gather.5.cloned.1.call-start = ((), (), s32[]{:S(2)}) async-start(), calls=%async_computation.10 | async-start | bytes 2129920 | tf_op jit(solution)/shard_map/all_gather | solution.py:102
  10.7 91.0 %copy-start.17 = (f32[128]{0:T(128)}, f32[128]{0:T(128)S(1)}, u32[]{:S(2)}) copy-start(f32[128]{0:T(128)S(1)} %get-tuple-element.27) | copy-start | bytes 1540
  11.5 90.2 %copy-start = (bf16[128,4096]{1,0:T(8,128)(2,1)S(1)}, bf16[128,4096]{1,0:T(8,128)(2,1)}, u32[]{:S(2)}) copy-start(bf16[128,4096]{1,0:T(8,128)(2,1)} %param.8) | copy-start | bytes 3145732
  11.5 90.2 %copy-start.13 = (f32[4096]{0:T(1024)S(1)}, f32[4096]{0:T(1024)}, u32[]{:S(2)}) copy-start(f32[4096]{0:T(1024)} %param.9) | copy-start | bytes 49156
  106.7 7.2 %collective-permute-start = (bf16[2,3,256]{2,0,1:T(2,128)(2,1)S(1)}, bf16[2,3,256]{2,0,1:T(2,128)(2,1)S(1)}, u32[]{:S(2)}, u32[]{:S(2)}) collective-permute-start(bf16[2,3,256]{2,0,1:T(2,128)(2,1)S(1)} %bitcast.268), channel_id=1, source_target_pairs={{0,4},{4,8},{8,12},{12,16},{16,20},{20,24},{24,28},{28,32},{32,36}... | collective-permute-start | bytes 9224 | tf_op jit(solution)/shard_map/ppermute | solution.py:15
  109.4 61.1 %copy-start.4 = (bf16[128,4096]{1,0:T(8,128)(2,1)S(1)}, bf16[128,4096]{1,0:T(8,128)(2,1)}, u32[]{:S(2)}) copy-start(bf16[128,4096]{1,0:T(8,128)(2,1)} %param.15) | copy-start | bytes 3145732
  115.0 58.1 %copy-start.12 = (f32[128,256]{1,0:T(8,128)S(1)}, f32[128,256]{1,0:T(8,128)}, u32[]{:S(2)}) copy-start(f32[128,256]{1,0:T(8,128)} %param.12) | copy-start | bytes 393220
  115.0 59.3 %all-to-all-start = ((f32[2,1,128,256]{3,0,1,2:T(2,128)}), f32[2,1,128,256]{3,0,1,2:T(2,128)S(1)}, u32[]{:S(2)}, u32[]{:S(2)}) async-start(f32[2,1,128,256]{3,0,1,2:T(2,128)} %copy.106), calls=%async_computation | async-start | bytes 524288 | tf_op jit(solution)/shard_map/all_to_all | solution.py:19
  174.3 22.0 %all-to-all-start.4 = ((f32[3,1,128,256]{3,1,0,2:T(1,128)}), f32[3,1,128,256]{3,1,0,2:T(1,128)}, u32[]{:S(2)}, u32[]{:S(2)}) async-start(f32[3,1,128,256]{3,1,0,2:T(1,128)} %copy.118), calls=%async_computation.5 | async-start | bytes 786432 | tf_op jit(solution)/shard_map/all_to_all | solution.py:19
  196.3 47.2 %all-to-all-start.1 = ((f32[4,2,128,256]{3,1,0,2:T(2,128)}), f32[4,2,128,256]{3,1,0,2:T(2,128)}, u32[]{:S(2)}, u32[]{:S(2)}) async-start(f32[4,2,128,256]{3,1,0,2:T(2,128)} %copy.110), calls=%async_computation.1 | async-start | bytes 2097152 | tf_op jit(solution)/shard_map/all_to_all | solution.py:19
  243.5 46.2 %all-to-all-start.5 = ((f32[6,2,128,256]{3,1,0,2:T(2,128)}), f32[6,2,128,256]{3,1,0,2:T(2,128)S(1)}, u32[]{:S(2)}, u32[]{:S(2)}) async-start(f32[6,2,128,256]{3,1,0,2:T(2,128)} %copy.123), calls=%async_computation.6 | async-start | bytes 3145728 | tf_op jit(solution)/shard_map/all_to_all | solution.py:19
  289.8 27.4 %all-to-all-start.2 = ((f32[2,2,128,256]{3,1,0,2:T(2,128)}), f32[2,2,128,256]{3,1,0,2:T(2,128)}, u32[]{:S(2)}, u32[]{:S(2)}) async-start(f32[2,2,128,256]{3,1,0,2:T(2,128)} %copy.114), calls=%async_computation.2 | async-start | bytes 1048576 | tf_op jit(solution)/shard_map/all_to_all | solution.py:19
  317.2 37.3 %all-to-all-start.6 = ((f32[4,2,128,256]{3,1,0,2:T(2,128)}), f32[4,2,128,256]{3,1,0,2:T(2,128)S(1)}, u32[]{:S(2)}, u32[]{:S(2)}) async-start(f32[4,2,128,256]{3,1,0,2:T(2,128)} %copy.128), calls=%async_computation.7 | async-start | bytes 2097152 | tf_op jit(solution)/shard_map/all_to_all | solution.py:19
  354.5 17.5 %all-to-all-start.3 = ((f32[1,2,64,256]{3,1,0,2:T(2,128)}), f32[1,2,64,256]{3,1,0,2:T(2,128)}, u32[]{:S(2)}, u32[]{:S(2)}) async-start(f32[1,2,64,256]{3,1,0,2:T(2,128)} %copy.117), calls=%async_computation.3 | async-start | bytes 262144 | tf_op jit(solution)/shard_map/all_to_all | solution.py:19
  364.9 29.9 %copy-start.1 = (bf16[256,4096]{0,1:T(8,128)(2,1)S(1)}, bf16[256,4096]{0,1:T(8,128)(2,1)}, u32[]{:S(2)}) copy-start(bf16[256,4096]{0,1:T(8,128)(2,1)} %all-gather.5.cloned.1.call-done) | copy-start | bytes 6291460
  371.9 17.6 %all-to-all-start.7 = ((f32[2,2,64,256]{3,1,0,2:T(2,128)}), f32[2,2,64,256]{3,1,0,2:T(2,128)}, u32[]{:S(2)}, u32[]{:S(2)}) async-start(f32[2,2,64,256]{3,1,0,2:T(2,128)} %copy.132), calls=%async_computation.8 | async-start | bytes 524288 | tf_op jit(solution)/shard_map/all_to_all | solution.py:19
  378.1 42.3 %reduce-scatter.2.cloned.1.call-start = ((), (), s32[]{:S(2)}) async-start(), calls=%async_computation.11 | async-start | bytes 1310720 | tf_op jit(solution)/shard_map/reduce_scatter | solution.py:126
  396.7 89.5 %all-reduce.2.cloned.1.call-start = ((), (), s32[]{:S(2)}) async-start(), calls=%async_computation.12 | async-start | bytes 4194304 | tf_op jit(solution)/shard_map/psum | solution.py:156
  398.7 4.3 collective-permute-start.1
  409.6 76.6 %copy-start.14 = (f32[4096]{0:T(1024)S(1)}, f32[4096]{0:T(1024)}, u32[]{:S(2)}) copy-start(f32[4096]{0:T(1024)} %param.9) | copy-start | bytes 49156
  411.9 76.4 %copy-start.5 = (bf16[128,4096]{1,0:T(8,128)(2,1)S(1)}, bf16[128,4096]{1,0:T(8,128)(2,1)}, u32[]{:S(2)}) copy-start(bf16[128,4096]{1,0:T(8,128)(2,1)} %param.15) | copy-start | bytes 3145732
  411.9 76.4 %copy-start.16 = (f32[128]{0:T(128)S(1)}, f32[128]{0:T(128)}, u32[]{:S(2)}) copy-start(f32[128]{0:T(128)} %get-tuple-element.26) | copy-start | bytes 1540
  411.9 76.4 %copy-start.18 = (f32[128]{0:T(128)S(1)}, f32[128]{0:T(128)}, u32[]{:S(2)}) copy-start(f32[128]{0:T(128)} %copy-done.17) | copy-start | bytes 1540
  (9 other events, 58.1 us)
Sparse Core Ops, SparseCore 0:
  10.8 82.1 all-gather.2
  95.8 74.5 all-gather.4
  396.8 23.5 reduce-scatter.1
  422.6 63.5 all-reduce.1
where the time goes:
time: 507 us; the launch traced here: 497 us
  waiting for transfers between devices  297 us (59%)
  starting transfers between devices  80.5 us (16%)
  local copies, waits for them, and re-layouts  43.7 us (9%)
  matrix products  43.5 us (9%)
  other arithmetic  17.6 us (3%)
  between operations  14.7 us (3%)
    all_to_all x8, waiting for transfers between devices, regroup(): return lax.all_to_all(data, 'seq', split_axis=2, concat_axis=1, tiled=True)  87.1 us
    all_gather x1, waiting for transfers between devices, per_device(): lax.all_gather(in_weight, 'seq', axis=0, tiled=True)  81.5 us
    all_to_all x8, starting transfers between devices, regroup(): return lax.all_to_all(data, 'seq', split_axis=2, concat_axis=1, tiled=True)  75.1 us
    psum x1, waiting for transfers between devices, per_device(): norm_grad = lax.psum(partial_grad, 'ch')  63.9 us
    all_gather x1, waiting for transfers between devices, per_device(): lax.all_gather(out_weight, 'seq', axis=1, tiled=True)  49 us
  transfers between devices with their start and end apart: 14, of which 12 were waited for; matrix products, arithmetic and copies ran while one was open for 19% of the time, Pallas kernels for 0%

commit v1 on v0

v1 whole, which is shorter than its diff:
```python
import math

import jax
import jax.numpy as jnp
from jax import lax
from jax.sharding import PartitionSpec as P

epsilon = 1e-05
highest = lax.Precision.HIGHEST


def passed_along(block, axis, distance):
    devices = range(lax.axis_size(axis))
    route = [(i - distance, i) for i in devices if i - distance in devices]
    return lax.ppermute(block, axis, route)


def to_columns(signals):
    return lax.all_to_all(signals, "seq", split_axis=1, concat_axis=2, tiled=True)


def to_rows(signals):
    return lax.all_to_all(signals, "seq", split_axis=2, concat_axis=1, tiled=True)


def turn_table(rows, cols, period, sign):
    turns = jnp.arange(rows, dtype=jnp.int32)[:, None] * jnp.arange(cols, dtype=jnp.int32)[None, :]
    phases = sign * 2.0 * math.pi / period * (turns % period).astype(jnp.float32)
    return (jnp.cos(phases), jnp.sin(phases))


def fft_sizes(seq_total):
    total = 2 * seq_total
    inner = 1
    while inner * inner < total:
        inner *= 2
    return total // inner, inner


def forward_dft(signals):
    count, chans, seq_total = signals.shape
    outer, inner = fft_sizes(seq_total)
    grid = signals.reshape(count, chans, outer // 2, inner)
    cos_out, sin_out = turn_table(outer, outer // 2, outer, 1.0)
    first_real = jnp.einsum("kn,ucnm->uckm", cos_out, grid, precision=highest)
    first_imag = -jnp.einsum("kn,ucnm->uckm", sin_out, grid, precision=highest)
    cos_tw, sin_tw = turn_table(outer, inner, outer * inner, 1.0)
    turned_real = first_real * cos_tw + first_imag * sin_tw
    turned_imag = first_imag * cos_tw - first_real * sin_tw
    cos_in, sin_in = turn_table(inner, inner, inner, 1.0)
    spec_real = jnp.einsum("uckm,mj->uckj", turned_real, cos_in, precision=highest) + jnp.einsum(
        "uckm,mj->uckj", turned_imag, sin_in, precision=highest
    )
    spec_imag = jnp.einsum("uckm,mj->uckj", turned_imag, cos_in, precision=highest) - jnp.einsum(
        "uckm,mj->uckj", turned_real, sin_in, precision=highest
    )
    return spec_real, spec_imag


def inverse_dft(spec_real, spec_imag):
    count, chans, outer, inner = spec_real.shape
    cos_in, sin_in = turn_table(inner, inner, inner, 1.0)
    back_real = jnp.einsum("uckj,jm->uckm", spec_real, cos_in, precision=highest) - jnp.einsum(
        "uckj,jm->uckm", spec_imag, sin_in, precision=highest
    )
    back_imag = jnp.einsum("uckj,jm->uckm", spec_imag, cos_in, precision=highest) + jnp.einsum(
        "uckj,jm->uckm", spec_real, sin_in, precision=highest
    )
    cos_tw, sin_tw = turn_table(outer, inner, outer * inner, 1.0)
    turned_real = back_real * cos_tw - back_imag * sin_tw
    turned_imag = back_imag * cos_tw + back_real * sin_tw
    cos_out, sin_out = turn_table(outer, outer // 2, outer, 1.0)
    grid = jnp.einsum("kn,uckm->ucnm", cos_out, turned_real, precision=highest) - jnp.einsum(
        "kn,uckm->ucnm", sin_out, turned_imag, precision=highest
    )
    return grid.reshape(count, chans, outer * inner // 2) / float(outer * inner)


def per_device(
    inputs, norm_gain, in_weight, short_filter, long_filter, conv_bias, out_weight, out_grad
):
    local_rows = inputs.shape[0]
    model_width = inputs.shape[1]
    slab_width = long_filter.shape[1]
    taps = short_filter.shape[1]
    wide_inputs = inputs.astype(jnp.float32)
    inv_rms = lax.rsqrt(jnp.mean(wide_inputs * wide_inputs, axis=1, keepdims=True) + epsilon)
    normed = (wide_inputs * inv_rms * norm_gain).astype(jnp.bfloat16)
    in_panel, out_panel = (
        lax.all_gather(in_weight, "seq", axis=0, tiled=True),
        lax.all_gather(out_weight, "seq", axis=1, tiled=True),
    )
    in_flat = in_panel.reshape(model_width, 3 * slab_width)
    projected = jnp.dot(normed, in_flat, preferred_element_type=jnp.float32)
    projected = projected.astype(jnp.bfloat16).reshape(local_rows, 3, slab_width)
    upper_rim = passed_along(projected[local_rows - (taps - 1) :], "seq", 1)
    extended = jnp.concatenate([upper_rim, projected], 0).astype(jnp.float32)
    mixed = jnp.zeros((local_rows, 3, slab_width), jnp.float32)
    for offset in range(taps):
        begin = taps - 1 - offset
        mixed = mixed + short_filter[:, offset, :][None] * extended[begin : begin + local_rows]
    query_br = mixed[:, 0]
    key_br = mixed[:, 1]
    value_br = mixed[:, 2]
    product = key_br * value_br
    gate_grad = jnp.dot(out_grad, out_panel.T, preferred_element_type=jnp.float32)
    carried = gate_grad * query_br
    columns = to_columns(jnp.stack([product, long_filter, carried]).transpose(0, 2, 1))
    all_real, all_imag = forward_dft(columns)
    sig_real, filt_real, grad_real = (all_real[0], all_real[1], all_real[2])
    sig_imag, filt_imag, grad_imag = (all_imag[0], all_imag[1], all_imag[2])
    conv_real = sig_real * filt_real - sig_imag * filt_imag
    conv_imag = sig_real * filt_imag + sig_imag * filt_real
    back_real = grad_real * filt_real + grad_imag * filt_imag
    back_imag = grad_imag * filt_real - grad_real * filt_imag
    pair_real = grad_real * sig_real + grad_imag * sig_imag
    pair_imag = grad_imag * sig_real - grad_real * sig_imag
    outs = inverse_dft(
        jnp.stack([conv_real, back_real, pair_real]), jnp.stack([conv_imag, back_imag, pair_imag])
    )
    returned = to_rows(outs).transpose(0, 2, 1)
    conv_out = returned[0]
    back_conv = returned[1]
    filter_grad = returned[2] * float(local_rows * lax.axis_size("seq")) ** (-0.5)
    biased = conv_out + conv_bias * product
    gated = (query_br * biased).astype(jnp.bfloat16)
    partial_out = jnp.dot(gated, out_panel, preferred_element_type=jnp.float32)
    summed = lax.psum_scatter(
        partial_out.astype(jnp.bfloat16), "ch", scatter_dimension=1, tiled=True
    ).astype(jnp.float32)
    share = summed.shape[1]
    residual = lax.dynamic_slice_in_dim(wide_inputs, lax.axis_index("ch") * share, share, 1)
    block_out = (residual + summed).astype(jnp.bfloat16)
    source_grad = back_conv + conv_bias * carried
    mixed_grad = jnp.stack([gate_grad * biased, source_grad * value_br, source_grad * key_br], 1)
    lower_rim = passed_along(mixed_grad[: taps - 1], "seq", -1)
    extended_back = jnp.concatenate([mixed_grad, lower_rim], 0)
    proj_grad = jnp.zeros((local_rows, 3, slab_width), jnp.float32)
    for offset in range(taps):
        proj_grad = (
            proj_grad
            + short_filter[:, offset, :][None] * extended_back[offset : offset + local_rows]
        )
    proj_grad = proj_grad.astype(jnp.bfloat16).reshape(local_rows, 3 * slab_width)
    partial_grad = jnp.dot(proj_grad, in_flat.T, preferred_element_type=jnp.float32)
    norm_grad = lax.psum(partial_grad, "ch")
    weighted = norm_grad * norm_gain
    inner_term = jnp.mean(weighted * wide_inputs, axis=1, keepdims=True)
    in_grad = (
        out_grad.astype(jnp.float32) + weighted * inv_rms - wide_inputs * inv_rms**3 * inner_term
    ).astype(jnp.bfloat16)
    return (block_out, in_grad, filter_grad)


def solution(mesh):
    return jax.shard_map(
        per_device,
        mesh=mesh,
        in_specs=(
            P("seq", None),
            P(),
            P("seq", None, "ch"),
            P(None, None, "ch"),
            P("seq", "ch"),
            P("ch"),
            P("ch", "seq"),
            P("seq", None),
        ),
        out_specs=(P("seq", "ch"), P("seq", None), P("seq", "ch")),
        check_vma=False,
    )
```

time: 507 us -> 395 us (0.78); the launches traced: 497 us -> 393 us
  starting transfers between devices: 80.5 us -> 13.4 us
  waiting for transfers between devices: 297 us -> 233 us
  blocking collectives: 0 us -> 20.8 us
  local copies, waits for them, and re-layouts: 43.7 us -> 62.4 us
  matrix products: 43.5 us -> 31.5 us
    all_to_all x8 -> x1, waiting for transfers between devices: 87.1 us -> 15.7 us  [to_columns(): lax.all_to_all(signals, 'seq', split_axis=1, concat_axis=2, tiled=True)]
    all_to_all x8 -> x1, starting transfers between devices: 75.1 us -> 7.79 us  [to_columns(): lax.all_to_all(signals, 'seq', split_axis=1, concat_axis=2, tiled=True)]
    all_to_all x0 -> x1, blocking collectives: none -> 20.8 us  [to_rows(): lax.all_to_all(signals, 'seq', split_axis=2, concat_axis=1, tiled=True)]
    unnamed x45 -> x34, local copies, waits for them, and re-layouts: 7.55 us -> 28.1 us
    all_gather x1, waiting for transfers between devices: 49 us -> 61.2 us  [per_device(): lax.all_gather(out_weight, 'seq', axis=1, tiled=True)]
    dot_general x24 -> x12, matrix products: 28.2 us -> 16.4 us  [the longest x1 1.6 us: forward_dft(): jnp.einsum('uckm,mj->uckj', turned_imag, sin_in, precision=highest)]
    reshape x7 -> x0, local copies, waits for them, and re-layouts: 10.8 us -> none  [the longest x2 5.58 us: to_spectrum(): jnp.stack([real_part, imag_part], 1)]
    all_to_all x4, local copies, waits for them, and re-layouts: 4.34 us -> 14.6 us  [to_rows(): lax.all_to_all(signals, 'seq', split_axis=2, concat_axis=1, tiled=True)]
  transfers between devices with their start and end apart: 14 -> 7, of which waited for: 12 -> 6; matrix products, arithmetic and copies ran while one was open for 19% -> 8% of each run, Pallas kernels for 0% -> 0%
where the time goes in v1:
time: 395 us; the launch traced here: 393 us
  waiting for transfers between devices  233 us (59%)
  local copies, waits for them, and re-layouts  62.4 us (16%)
  matrix products  31.5 us (8%)
  blocking collectives  20.8 us (5%)
  other arithmetic  17.5 us (4%)
  between operations  14.1 us (4%)
  starting transfers between devices  13.4 us (3%)
    all_gather x1, waiting for transfers between devices, per_device(): lax.all_gather(in_weight, 'seq', axis=0, tiled=True)  81.4 us
    psum x1, waiting for transfers between devices, per_device(): norm_grad = lax.psum(partial_grad, 'ch')  64 us
    all_gather x1, waiting for transfers between devices, per_device(): lax.all_gather(out_weight, 'seq', axis=1, tiled=True)  61.2 us
    unnamed x34, local copies, waits for them, and re-layouts  28.1 us
    all_to_all x1, blocking collectives, to_rows(): lax.all_to_all(signals, 'seq', split_axis=2, concat_axis=1, tiled=True)  20.8 us
    all_to_all x1, waiting for transfers between devices, to_columns(): lax.all_to_all(signals, 'seq', split_axis=1, concat_axis=2, tiled=True)  15.7 us
    all_to_all x4, local copies, waits for them, and re-layouts, to_rows(): lax.all_to_all(signals, 'seq', split_axis=2, concat_axis=1, tiled=True)  14.6 us
    all_gather x1, local copies, waits for them, and re-layouts, per_device(): lax.all_gather(in_weight, 'seq', axis=0, tiled=True)  8.7 us
  transfers between devices with their start and end apart: 7, of which 6 were waited for; matrix products, arithmetic and copies ran while one was open for 8% of the time, Pallas kernels for 0%

profile of v1, /device:TPU:2, one launch (start us, length us, event | category | flops | bytes accessed | tf_op | source)
XLA Modules:
  0.0 392.8 jit_solution(6677568835043596494)
XLA Ops:
  11.6 81.4 %all-gather.3.cloned.1.call-done = bf16[4096,3,256]{2,0,1:T(8,128)(2,1)} async-done(((bf16[64,3,256]{2,0,1:T(8,128)(2,1)}), bf16[4096,3,256]{2,0,1:T(8,128)(2,1)}) %all-gather.3.cloned.1.call-update) | async-done | bytes 6291472 | tf_op jit(solution)/shard_map/all_gather | solution.py:90
  93.0 8.7 %copy.46 = bf16[4096,3,256]{0,2,1:T(8,128)(2,1)} copy(bf16[4096,3,256]{2,0,1:T(8,128)(2,1)} %all-gather.3.cloned.1.call-done) | data formatting | bytes 12582912 | tf_op jit(solution)/shard_map/all_gather | solution.py:90
  101.7 5.1 %convolution_convert_fusion.1 = bf16[128,768]{1,0:T(8,128)(2,1)S(1)} fusion(bf16[4096,768]{0,1:T(8,128)(2,1)} %bitcast.127, bf16[128,4096]{1,0:T(8,128)(2,1)S(1)} %copy-done, f32[4096]{0:T(1024)S(1)} %copy-done.9, f32[128]{0:T(128)S(1)} %get-tuple-element.19), kind=kOutput, calls=%fused_computation.16 | convolution fusion | flops 807501824 | bytes 7553536 | tf_op jit(solution)/shard_map/dot_general | solution.py:94
  106.8 2.1 collective-permute-start
  109.0 61.2 %all-gather.5.cloned.1.call-done = bf16[256,4096]{0,1:T(8,128)(2,1)} async-done(((bf16[256,64]{0,1:T(8,128)(2,1)}), bf16[256,4096]{0,1:T(8,128)(2,1)}) %all-gather.5.cloned.1.call-update) | async-done | bytes 2097168 | tf_op jit(solution)/shard_map/all_gather | solution.py:91
  170.2 2.0 fusion.143
  174.2 7.8 %all-to-all-start = ((f32[3,256,128]{2,0,1:T(4,128)}), f32[3,256,128]{2,0,1:T(4,128)S(1)}, u32[]{:S(2)}, u32[]{:S(2)}) async-start(f32[3,256,128]{2,0,1:T(4,128)} %copy.50), calls=%async_computation | async-start | bytes 1048576 | tf_op jit(solution)/shard_map/all_to_all | solution.py:19
  183.0 15.7 %all-to-all-done = f32[3,256,128]{2,0,1:T(4,128)S(1)} async-done(((f32[3,256,128]{2,0,1:T(4,128)}), f32[3,256,128]{2,0,1:T(4,128)S(1)}, u32[]{:S(2)}, u32[]{:S(2)}) %all-to-all-start) | async-done | bytes 393248 | tf_op jit(solution)/shard_map/all_to_all | solution.py:19
  215.4 8.6 %copy.85 = f32[3,4,64,128]{1,0,3,2:T(4,128)} copy(f32[3,4,64,128]{3,2,1,0:T(8,128)S(1)} %fusion.2) | data formatting | bytes 786432 | tf_op jit(solution)/shard_map/div | solution.py:76
  224.0 16.0 %reshape.105 = f32[64,1,1536]{2,1,0:T(1,128)S(1)} reshape(f32[8192,3,4]{2,1,0:T(4,128)} %bitcast.125) | data formatting | bytes 786432
  240.1 20.8 %all_to_all.33 = f32[64,1,1536]{2,1,0:T(1,128)S(1)} all-to-all(f32[64,1,1536]{2,1,0:T(1,128)S(1)} %reshape.105), channel_id=1, replica_groups=mesh['seq'=64,'ch'=4] {'seq'}, dimensions={0} | all-to-all | bytes 786432 | tf_op jit(solution)/shard_map/all_to_all | solution.py:23
  262.9 11.6 %reshape.106 = f32[8192,3,4]{2,1,0:T(4,128)} reshape(f32[64,1536]{1,0:T(8,128)S(1)} %reduce) | data formatting | bytes 786432
  274.5 10.1 %copy.86 = f32[3,4,64,128]{3,2,1,0:T(8,128)} copy(f32[3,4,64,128]{1,0,3,2:T(4,128)} %bitcast.126) | data formatting | bytes 786432 | tf_op jit(solution)/shard_map/all_to_all | solution.py:23
  284.6 2.2 copy.67
  286.7 1.9 copy.68
  288.6 1.8 fusion.37
  290.4 1.8 convolution_convert_fusion
  294.3 3.1 collective-permute-start.1
  298.5 6.2 %convolution_bitcast_fusion = f32[128,4096]{1,0:T(8,128)} fusion(bf16[4096,3,256]{2,0,1:T(8,128)(2,1)} %all-gather.3.cloned.1.call-done, f32[130,3,256]{2,0,1:T(8,128)S(1)} %pad_maximum_fusion.6, f32[3,256]{1,0:T(4,128)S(1)} %get-tuple-element.20, f32[3,256]{1,0:T(4,128)S(1)} %get-tuple-element.21, f32[3,256]{1,0:T(4,128)S(1)} %bitcast.136, ...), kind=kOutput, calls=%fused_computation | convolution fusion | flops 806092800 | bytes 9580544 | tf_op jit(solution)/shard_map/dot_general | solution.py:145
  307.9 8.3 %reduce-scatter.2.cloned.1.call-done = bf16[128,1024]{1,0:T(8,128)(2,1)} async-done(((bf16[128,4096]{1,0:T(8,128)(2,1)}), bf16[128,1024]{1,0:T(8,128)(2,1)}) %reduce-scatter.2.cloned.1.call-update) | async-done | bytes 262160 | tf_op jit(solution)/shard_map/reduce_scatter | solution.py:128
  316.2 1.9 add_convert_fusion
  318.1 64.0 %all-reduce.2.cloned.1.call-done = f32[128,4096]{1,0:T(8,128)} async-done(((f32[128,4096]{1,0:T(8,128)}), f32[128,4096]{1,0:T(8,128)}) %all-reduce.2.cloned.1.call-update) | async-done | bytes 2097168 | tf_op jit(solution)/shard_map/psum | solution.py:146
  382.1 2.1 multiply_reduce_fusion
  384.3 1.9 subtract_convert_fusion
  (81 shorter events, 32.3 us)
Async XLA Ops:
  7.2 85.9 %all-gather.3.cloned.1.call-start = ((), (), s32[]{:S(2)}) async-start(), calls=%async_computation.3 | async-start | bytes 6389760 | tf_op jit(solution)/shard_map/all_gather | solution.py:90
  7.9 162.3 %all-gather.5.cloned.1.call-start = ((), (), s32[]{:S(2)}) async-start(), calls=%async_computation.4 | async-start | bytes 2129920 | tf_op jit(solution)/shard_map/all_gather | solution.py:91
  11.6 90.1 %copy-start.13 = (f32[128]{0:T(128)}, f32[128]{0:T(128)S(1)}, u32[]{:S(2)}) copy-start(f32[128]{0:T(128)S(1)} %get-tuple-element.19) | copy-start | bytes 1540
  11.6 90.1 %copy-start = (bf16[128,4096]{1,0:T(8,128)(2,1)S(1)}, bf16[128,4096]{1,0:T(8,128)(2,1)}, u32[]{:S(2)}) copy-start(bf16[128,4096]{1,0:T(8,128)(2,1)} %param.8) | copy-start | bytes 3145732
  11.6 90.1 %copy-start.9 = (f32[4096]{0:T(1024)S(1)}, f32[4096]{0:T(1024)}, u32[]{:S(2)}) copy-start(f32[4096]{0:T(1024)} %param.9) | copy-start | bytes 49156
  101.7 68.5 %copy-start.3 = (bf16[128,4096]{1,0:T(8,128)(2,1)S(1)}, bf16[128,4096]{1,0:T(8,128)(2,1)}, u32[]{:S(2)}) copy-start(bf16[128,4096]{1,0:T(8,128)(2,1)} %param.15) | copy-start | bytes 3145732
  106.8 65.7 %collective-permute-start = (bf16[2,3,256]{2,0,1:T(2,128)(2,1)S(1)}, bf16[2,3,256]{2,0,1:T(2,128)(2,1)S(1)}, u32[]{:S(2)}, u32[]{:S(2)}) collective-permute-start(bf16[2,3,256]{2,0,1:T(2,128)(2,1)S(1)} %bitcast.138), channel_id=1, source_target_pairs={{0,4},{4,8},{8,12},{12,16},{16,20},{20,24},{24,28},{28,32},{32,36}... | collective-permute-start | bytes 9224 | tf_op jit(solution)/shard_map/ppermute | solution.py:15
  172.2 1.0 copy-start.7
  172.2 1.0 copy-start.8
  174.2 24.5 %all-to-all-start = ((f32[3,256,128]{2,0,1:T(4,128)}), f32[3,256,128]{2,0,1:T(4,128)S(1)}, u32[]{:S(2)}, u32[]{:S(2)}) async-start(f32[3,256,128]{2,0,1:T(4,128)} %copy.50), calls=%async_computation | async-start | bytes 1048576 | tf_op jit(solution)/shard_map/all_to_all | solution.py:19
  182.0 134.2 %reduce-scatter.2.cloned.1.call-start = ((), (), s32[]{:S(2)}) async-start(), calls=%async_computation.5 | async-start | bytes 1310720 | tf_op jit(solution)/shard_map/reduce_scatter | solution.py:128
  274.5 14.1 %copy-start.11 = (f32[256]{0:T(256)S(1)}, f32[256]{0:T(256)}, u32[]{:S(2)}) copy-start(f32[256]{0:T(256)} %param.13) | copy-start | bytes 3076
  284.6 5.9 %copy-start.1 = (bf16[256,4096]{0,1:T(8,128)(2,1)S(1)}, bf16[256,4096]{0,1:T(8,128)(2,1)}, u32[]{:S(2)}) copy-start(bf16[256,4096]{0,1:T(8,128)(2,1)} %all-gather.5.cloned.1.call-done) | copy-start | bytes 6291460
  292.2 6.3 %copy-start.5 = (f32[128,1,256]{2,0,1:T(8,128)S(1)}, f32[128,1,256]{2,0,1:T(8,128)}, u32[]{:S(2)}) copy-start(f32[128,1,256]{2,0,1:T(8,128)} %get-tuple-element.5) | copy-start | bytes 393220
  292.2 6.3 %copy-start.6 = (f32[128,1,256]{2,0,1:T(8,128)S(1)}, f32[128,1,256]{2,0,1:T(8,128)}, u32[]{:S(2)}) copy-start(f32[128,1,256]{2,0,1:T(8,128)} %get-tuple-element.13) | copy-start | bytes 393220
  292.3 89.8 %all-reduce.2.cloned.1.call-start = ((), (), s32[]{:S(2)}) async-start(), calls=%async_computation.6 | async-start | bytes 4194304 | tf_op jit(solution)/shard_map/psum | solution.py:146
  294.3 4.2 %collective-permute-start.1 = (f32[2,3,256]{2,0,1:T(2,128)S(1)}, f32[2,3,256]{2,0,1:T(2,128)S(1)}, u32[]{:S(2)}, u32[]{:S(2)}) collective-permute-start(f32[2,3,256]{2,0,1:T(2,128)S(1)} %slice.110), channel_id=1, source_target_pairs={{4,0},{8,4},{12,8},{16,12},{20,16},{24,20},{28,24},{32,28},{36,32}... | collective-permute-start | bytes 18440 | tf_op jit(solution)/shard_map/ppermute | solution.py:15
  304.8 77.3 %copy-start.10 = (f32[4096]{0:T(1024)S(1)}, f32[4096]{0:T(1024)}, u32[]{:S(2)}) copy-start(f32[4096]{0:T(1024)} %param.9) | copy-start | bytes 49156
  307.9 76.3 %copy-start.4 = (bf16[128,4096]{1,0:T(8,128)(2,1)S(1)}, bf16[128,4096]{1,0:T(8,128)(2,1)}, u32[]{:S(2)}) copy-start(bf16[128,4096]{1,0:T(8,128)(2,1)} %param.15) | copy-start | bytes 3145732
  307.9 76.3 %copy-start.12 = (f32[128]{0:T(128)S(1)}, f32[128]{0:T(128)}, u32[]{:S(2)}) copy-start(f32[128]{0:T(128)} %get-tuple-element.18) | copy-start | bytes 1540
  307.9 76.3 %copy-start.14 = (f32[128]{0:T(128)S(1)}, f32[128]{0:T(128)}, u32[]{:S(2)}) copy-start(f32[128]{0:T(128)} %copy-done.13) | copy-start | bytes 1540
  382.1 2.2 copy-start.2
Sparse Core Ops, SparseCore 0:
  10.8 82.1 all-gather.2
  95.8 74.3 all-gather.4
  292.4 23.7 reduce-scatter.1
  318.4 63.6 all-reduce.1

commit v2 on v1

--- a/solution.py
+++ b/solution.py
@@ -20,7 +20,12 @@
 
 
 def to_rows(signals):
-    return lax.all_to_all(signals, "seq", split_axis=2, concat_axis=1, tiled=True)
+    count, chans, seq_total = signals.shape
+    devices = lax.axis_size("seq")
+    local_rows = seq_total // devices
+    pieces = signals.reshape(count, chans, devices, local_rows).transpose(2, 0, 1, 3)
+    arrived = lax.all_to_all(pieces, "seq", split_axis=0, concat_axis=0, tiled=True)
+    return arrived.transpose(1, 3, 0, 2).reshape(count, local_rows, devices * chans)
 
 
 def turn_table(rows, cols, period, sign):
@@ -118,7 +123,7 @@
     outs = inverse_dft(
         jnp.stack([conv_real, back_real, pair_real]), jnp.stack([conv_imag, back_imag, pair_imag])
     )
-    returned = to_rows(outs).transpose(0, 2, 1)
+    returned = to_rows(outs)
     conv_out = returned[0]
     back_conv = returned[1]
     filter_grad = returned[2] * float(local_rows * lax.axis_size("seq")) ** (-0.5)
@@ -143,12 +148,20 @@
         )
     proj_grad = proj_grad.astype(jnp.bfloat16).reshape(local_rows, 3 * slab_width)
     partial_grad = jnp.dot(proj_grad, in_flat.T, preferred_element_type=jnp.float32)
-    norm_grad = lax.psum(partial_grad, "ch")
-    weighted = norm_grad * norm_gain
-    inner_term = jnp.mean(weighted * wide_inputs, axis=1, keepdims=True)
-    in_grad = (
-        out_grad.astype(jnp.float32) + weighted * inv_rms - wide_inputs * inv_rms**3 * inner_term
+    norm_grad = lax.psum_scatter(
+        partial_grad.astype(jnp.bfloat16), "ch", scatter_dimension=1, tiled=True
+    ).astype(jnp.float32)
+    feature_share = norm_grad.shape[1]
+    feature_begin = lax.axis_index("ch") * feature_share
+    gain_share = lax.dynamic_slice_in_dim(norm_gain, feature_begin, feature_share, 0)
+    inputs_share = lax.dynamic_slice_in_dim(wide_inputs, feature_begin, feature_share, 1)
+    grad_share = lax.dynamic_slice_in_dim(out_grad, feature_begin, feature_share, 1)
+    weighted = norm_grad * gain_share
+    inner_term = lax.psum(jnp.sum(weighted * inputs_share, axis=1, keepdims=True), "ch") / model_width
+    in_grad_share = (
+        grad_share.astype(jnp.float32) + weighted * inv_rms - inputs_share * inv_rms**3 * inner_term
     ).astype(jnp.bfloat16)
+    in_grad = lax.all_gather(in_grad_share, "ch", axis=1, tiled=True)
     return (block_out, in_grad, filter_grad)
 
 

time: 395 us -> 340 us (0.86)
  local copies, waits for them, and re-layouts: 62.4 us -> 15.6 us
  other arithmetic: 17.5 us -> 7.48 us
  blocking collectives: 20.8 us -> 29 us
  waiting for transfers between devices: 233 us -> 228 us
    psum x1 -> x0, waiting for transfers between devices: 64 us -> none  [per_device(): norm_grad = lax.psum(partial_grad, 'ch')]
    all_gather x0 -> x1, waiting for transfers between devices: none -> 25.8 us  [per_device(): in_grad = lax.all_gather(in_grad_share, 'ch', axis=1, tiled=True)]
    unnamed x34 -> x22, local copies, waits for them, and re-layouts: 28.1 us -> 3.43 us
    reduce_scatter x0 -> x1, waiting for transfers between devices: none -> 21.5 us  [per_device(): lax.psum_scatter(partial_grad.astype(jnp.bfloat16), 'ch', scatter_dimensi...]
    all_to_all x4 -> x0, local copies, waits for them, and re-layouts: 14.6 us -> none  [to_rows(): lax.all_to_all(signals, 'seq', split_axis=2, concat_axis=1, tiled=True)]
    reduce_scatter x1, waiting for transfers between devices: 8.26 us -> 19.2 us  [per_device(): lax.psum_scatter(partial_out.astype(jnp.bfloat16), 'ch', scatter_dimensio...]
    div x1, local copies, waits for them, and re-layouts: 8.64 us -> 0.26 us  [inverse_dft(): return grid.reshape(count, chans, outer * inner // 2) / float(outer * inner)]
    psum x0 -> x1, blocking collectives: none -> 8.2 us  [per_device(): lax.psum(jnp.sum(weighted * inputs_share, axis=1, keepdims=True), 'ch')]
  transfers between devices with their start and end apart: 7 -> 8, of which waited for: 6 -> 7; matrix products, arithmetic and copies ran while one was open for 8% -> 7% of each run, Pallas kernels for 0% -> 0%
where the time goes in v2:
time: 340 us
  waiting for transfers between devices  228 us (67%)
  matrix products  32.1 us (9%)
  blocking collectives  29 us (9%)
  local copies, waits for them, and re-layouts  15.6 us (5%)
  between operations  14.2 us (4%)
  starting transfers between devices  13.2 us (4%)
  other arithmetic  7.48 us (2%)
    all_gather x1, waiting for transfers between devices, per_device(): lax.all_gather(in_weight, 'seq', axis=0, tiled=True)  82 us
    all_gather x1, waiting for transfers between devices, per_device(): lax.all_gather(out_weight, 'seq', axis=1, tiled=True)  61.2 us
    all_gather x1, waiting for transfers between devices, per_device(): in_grad = lax.all_gather(in_grad_share, 'ch', axis=1, tiled=True)  25.8 us
    reduce_scatter x1, waiting for transfers between devices, per_device(): lax.psum_scatter(partial_grad.astype(jnp.bfloat16), 'ch', scatter_dimensi...  21.5 us
    all_to_all x1, blocking collectives, to_rows(): lax.all_to_all(pieces, 'seq', split_axis=0, concat_axis=0, tiled=True)  20.8 us
    reduce_scatter x1, waiting for transfers between devices, per_device(): lax.psum_scatter(partial_out.astype(jnp.bfloat16), 'ch', scatter_dimensio...  19.2 us
    all_to_all x1, waiting for transfers between devices, to_columns(): lax.all_to_all(signals, 'seq', split_axis=1, concat_axis=2, tiled=True)  15.7 us
    all_gather x1, local copies, waits for them, and re-layouts, per_device(): lax.all_gather(in_weight, 'seq', axis=0, tiled=True)  8.72 us
  transfers between devices with their start and end apart: 8, of which 7 were waited for; matrix products, arithmetic and copies ran while one was open for 7% of the time, Pallas kernels for 0%

profile of v2, /device:TPU:2, one launch (start us, length us, event | category | flops | bytes accessed | tf_op | source)
XLA Modules:
  0.0 339.6 jit_solution(12435328371923246589)
XLA Ops:
  9.5 1.5 multiply_reduce_fusion
  11.1 82.0 %all-gather.4.cloned.1.call-done = bf16[4096,3,256]{2,0,1:T(8,128)(2,1)} async-done(((bf16[64,3,256]{2,0,1:T(8,128)(2,1)}), bf16[4096,3,256]{2,0,1:T(8,128)(2,1)}) %all-gather.4.cloned.1.call-update) | async-done | bytes 6291472 | tf_op jit(solution)/shard_map/all_gather | solution.py:95
  93.0 8.7 %copy.52 = bf16[4096,3,256]{0,2,1:T(8,128)(2,1)} copy(bf16[4096,3,256]{2,0,1:T(8,128)(2,1)} %all-gather.4.cloned.1.call-done) | data formatting | bytes 12582912 | tf_op jit(solution)/shard_map/all_gather | solution.py:95
  101.8 5.1 %convolution_convert_fusion.1 = bf16[128,768]{1,0:T(8,128)(2,1)S(1)} fusion(bf16[4096,768]{0,1:T(8,128)(2,1)} %bitcast.113, f32[4096]{0:T(1024)S(1)} %copy-done.5, f32[128]{0:T(128)S(1)} %get-tuple-element.30, bf16[128,4096]{1,0:T(8,128)(2,1)S(1)} %copy-done.1), kind=kOutput, calls=%fused_computation.14 | convolution fusion | flops 807501824 | bytes 7553536 | tf_op jit(solution)/shard_map/dot_general | solution.py:99
  106.9 2.1 collective-permute-start
  109.0 61.2 %all-gather.6.cloned.1.call-done = bf16[256,4096]{0,1:T(8,128)(2,1)} async-done(((bf16[256,64]{0,1:T(8,128)(2,1)}), bf16[256,4096]{0,1:T(8,128)(2,1)}) %all-gather.6.cloned.1.call-update) | async-done | bytes 2097168 | tf_op jit(solution)/shard_map/all_gather | solution.py:96
  170.2 2.0 fusion.141
  174.2 7.8 %all-to-all-start = ((f32[3,256,128]{2,0,1:T(4,128)}), f32[3,256,128]{2,0,1:T(4,128)S(1)}, u32[]{:S(2)}, u32[]{:S(2)}) async-start(f32[3,256,128]{2,0,1:T(4,128)} %copy.56), calls=%async_computation | async-start | bytes 1048576 | tf_op jit(solution)/shard_map/all_to_all | solution.py:19
  182.9 15.7 %all-to-all-done = f32[3,256,128]{2,0,1:T(4,128)S(1)} async-done(((f32[3,256,128]{2,0,1:T(4,128)}), f32[3,256,128]{2,0,1:T(4,128)S(1)}, u32[]{:S(2)}, u32[]{:S(2)}) %all-to-all-start) | async-done | bytes 393248 | tf_op jit(solution)/shard_map/all_to_all | solution.py:19
  200.1 1.5 fusion.1
  201.6 1.6 fusion.32
  203.2 1.6 fusion.33
  204.8 1.6 convolution_add_fusion.1
  206.4 1.6 convolution_subtract_fusion.1
  215.5 20.8 %all_to_all.20 = f32[64,3,4,128]{3,2,1,0:T(4,128)S(1)} all-to-all(f32[64,3,4,128]{3,2,1,0:T(4,128)S(1)} %copy.71), channel_id=1, replica_groups=mesh['seq'=64,'ch'=4] {'seq'}, dimensions={0} | all-to-all | bytes 786432 | tf_op jit(solution)/shard_map/all_to_all | solution.py:27
  238.0 2.9 collective-permute-start.1
  242.2 6.1 %fusion = bf16[128,4096]{1,0:T(8,128)(2,1)} fusion(bf16[4096,3,256]{2,0,1:T(8,128)(2,1)} %all-gather.4.cloned.1.call-done, f32[130,3,256]{2,0,1:T(8,128)S(1)} %pad_maximum_fusion.6, f32[3,256]{1,0:T(4,128)S(1)} %get-tuple-element.31, f32[3,256]{1,0:T(4,128)S(1)} %get-tuple-element.32, f32[3,256]{1,0:T(4,128)S(1)} %bitcast.122, ...), kind=kOutput, calls=%fused_computation.1 | convolution fusion | flops 806617088 | bytes 8531968 | tf_op jit(solution)/shard_map/dot_general | solution.py:150
  248.4 2.7 convolution_convert_fusion
  252.1 21.5 %reduce-scatter.5.cloned.1.call-done = bf16[128,1024]{1,0:T(8,128)(2,1)} async-done(((bf16[128,4096]{1,0:T(8,128)(2,1)}), bf16[128,1024]{1,0:T(8,128)(2,1)}) %reduce-scatter.5.cloned.1.call-update) | async-done | bytes 262160 | tf_op jit(solution)/shard_map/reduce_scatter | solution.py:151
  274.7 8.2 %psum.7 = f32[128,1]{0,1:T(1,128)S(1)} all-reduce(f32[128,1]{0,1:T(1,128)S(1)} %bitcast.125), channel_id=1, replica_groups=mesh['seq'=64,'ch'=4] {'ch'}, use_global_device_ids=true, to_apply=%region_4.5 | all-reduce | flops 128 | bytes 1024 | tf_op jit(solution)/shard_map/psum | solution.py:160
  282.9 19.2 %reduce-scatter.3.cloned.1.call-done = bf16[128,1024]{1,0:T(8,128)(2,1)} async-done(((bf16[128,4096]{1,0:T(8,128)(2,1)}), bf16[128,1024]{1,0:T(8,128)(2,1)}) %reduce-scatter.3.cloned.1.call-update) | async-done | bytes 262160 | tf_op jit(solution)/shard_map/reduce_scatter | solution.py:133
  302.1 2.2 subtract_convert_fusion
  305.0 25.8 %all-gather.8.cloned.1.call-done = bf16[128,4096]{1,0:T(8,128)(2,1)} async-done(((bf16[128,1024]{1,0:T(8,128)(2,1)}), bf16[128,4096]{1,0:T(8,128)(2,1)}) %all-gather.8.cloned.1.call-update) | async-done | bytes 1048592 | tf_op jit(solution)/shard_map/all_gather | solution.py:164
  330.8 2.3 copy.107
  (70 shorter events, 19.9 us)
Async XLA Ops:
  7.2 85.9 %all-gather.4.cloned.1.call-start = ((), (), s32[]{:S(2)}) async-start(), calls=%async_computation.4 | async-start | bytes 6389760 | tf_op jit(solution)/shard_map/all_gather | solution.py:95
  7.9 162.3 %all-gather.6.cloned.1.call-start = ((), (), s32[]{:S(2)}) async-start(), calls=%async_computation.5 | async-start | bytes 2129920 | tf_op jit(solution)/shard_map/all_gather | solution.py:96
  11.0 90.7 %copy-start.7 = (f32[128]{0:T(128)}, f32[128]{0:T(128)S(1)}, u32[]{:S(2)}) copy-start(f32[128]{0:T(128)S(1)} %get-tuple-element.30) | copy-start | bytes 1540
  11.0 90.7 %copy-start.1 = (bf16[128,4096]{1,0:T(8,128)(2,1)S(1)}, bf16[128,4096]{1,0:T(8,128)(2,1)}, u32[]{:S(2)}) copy-start(bf16[128,4096]{1,0:T(8,128)(2,1)} %param.8) | copy-start | bytes 3145732
  11.1 90.7 %copy-start.5 = (f32[4096]{0:T(1024)S(1)}, f32[4096]{0:T(1024)}, u32[]{:S(2)}) copy-start(f32[4096]{0:T(1024)} %param.9) | copy-start | bytes 49156
  101.8 68.4 %copy-start.2 = (bf16[128,4096]{1,0:T(8,128)(2,1)S(1)}, bf16[128,4096]{1,0:T(8,128)(2,1)}, u32[]{:S(2)}) copy-start(bf16[128,4096]{1,0:T(8,128)(2,1)} %param.15) | copy-start | bytes 3145732
  106.9 65.7 %collective-permute-start = (bf16[2,3,256]{2,0,1:T(2,128)(2,1)S(1)}, bf16[2,3,256]{2,0,1:T(2,128)(2,1)S(1)}, u32[]{:S(2)}, u32[]{:S(2)}) collective-permute-start(bf16[2,3,256]{2,0,1:T(2,128)(2,1)S(1)} %bitcast.124), channel_id=1, source_target_pairs={{0,4},{4,8},{8,12},{12,16},{16,20},{20,24},{24,28},{28,32},{32,36}... | collective-permute-start | bytes 9224 | tf_op jit(solution)/shard_map/ppermute | solution.py:15
  172.2 0.9 copy-start.4
  174.2 24.5 %all-to-all-start = ((f32[3,256,128]{2,0,1:T(4,128)}), f32[3,256,128]{2,0,1:T(4,128)S(1)}, u32[]{:S(2)}, u32[]{:S(2)}) async-start(f32[3,256,128]{2,0,1:T(4,128)} %copy.56), calls=%async_computation | async-start | bytes 1048576 | tf_op jit(solution)/shard_map/all_to_all | solution.py:19
  182.0 91.6 %reduce-scatter.5.cloned.1.call-start = ((), (), s32[]{:S(2)}) async-start(), calls=%async_computation.7 | async-start | bytes 1310720 | tf_op jit(solution)/shard_map/reduce_scatter | solution.py:151
  214.1 23.1 %copy-start.6 = (f32[256]{0:T(256)S(1)}, f32[256]{0:T(256)}, u32[]{:S(2)}) copy-start(f32[256]{0:T(256)} %param.13) | copy-start | bytes 3076
  238.0 4.2 %collective-permute-start.1 = (f32[2,3,256]{2,0,1:T(2,128)S(1)}, f32[2,3,256]{2,0,1:T(2,128)S(1)}, u32[]{:S(2)}, u32[]{:S(2)}) collective-permute-start(f32[2,3,256]{2,0,1:T(2,128)S(1)} %slice.113), channel_id=1, source_target_pairs={{4,0},{8,4},{12,8},{16,12},{20,16},{24,20},{28,24},{32,28},{36,32}... | collective-permute-start | bytes 18440 | tf_op jit(solution)/shard_map/ppermute | solution.py:15
  242.2 6.1 %copy-start = (bf16[256,4096]{0,1:T(8,128)(2,1)S(1)}, bf16[256,4096]{0,1:T(8,128)(2,1)}, u32[]{:S(2)}) copy-start(bf16[256,4096]{0,1:T(8,128)(2,1)} %all-gather.6.cloned.1.call-done) | copy-start | bytes 6291460
  248.3 53.8 %reduce-scatter.3.cloned.1.call-start = ((), (), s32[]{:S(2)}) async-start(), calls=%async_computation.6 | async-start | bytes 1310720 | tf_op jit(solution)/shard_map/reduce_scatter | solution.py:133
  251.1 51.0 %copy-start.8 = (f32[128]{0:T(128)S(1)}, f32[128]{0:T(128)}, u32[]{:S(2)}) copy-start(f32[128]{0:T(128)} %copy-done.7) | copy-start | bytes 1540
  251.1 79.7 %all-gather.8.cloned.1.call-start = ((), (), s32[]{:S(2)}) async-start(), calls=%async_computation.8 | async-start | bytes 1310720 | tf_op jit(solution)/shard_map/all_gather | solution.py:164
  251.4 52.9 %copy-start.3 = (f32[1,128,64,4]{1,3,0,2:T(4,128)S(1)}, f32[1,128,64,4]{1,3,0,2:T(4,128)}, u32[]{:S(2)}) copy-start(f32[1,128,64,4]{1,3,0,2:T(4,128)} %get-tuple-element.23) | copy-start | bytes 393220
Sparse Core Ops, SparseCore 0:
  10.8 82.1 all-gather.3
  95.8 74.3 all-gather.5
  248.4 25.0 reduce-scatter.4
  276.0 26.0 reduce-scatter.2
  304.4 26.3 all-gather.7

commit v3 on v2

--- a/solution.py
+++ b/solution.py
@@ -7,6 +7,8 @@
 
 epsilon = 1e-05
 highest = lax.Precision.HIGHEST
+SEQ = ("chips", "core")
+CORES = 2
 
 
 def passed_along(block, axis, distance):
@@ -16,15 +18,15 @@
 
 
 def to_columns(signals):
-    return lax.all_to_all(signals, "seq", split_axis=1, concat_axis=2, tiled=True)
+    return lax.all_to_all(signals, SEQ, split_axis=1, concat_axis=2, tiled=True)
 
 
 def to_rows(signals):
     count, chans, seq_total = signals.shape
-    devices = lax.axis_size("seq")
+    devices = lax.axis_size(SEQ)
     local_rows = seq_total // devices
     pieces = signals.reshape(count, chans, devices, local_rows).transpose(2, 0, 1, 3)
-    arrived = lax.all_to_all(pieces, "seq", split_axis=0, concat_axis=0, tiled=True)
+    arrived = lax.all_to_all(pieces, SEQ, split_axis=0, concat_axis=0, tiled=True)
     return arrived.transpose(1, 3, 0, 2).reshape(count, local_rows, devices * chans)
 
 
@@ -91,14 +93,14 @@
     wide_inputs = inputs.astype(jnp.float32)
     inv_rms = lax.rsqrt(jnp.mean(wide_inputs * wide_inputs, axis=1, keepdims=True) + epsilon)
     normed = (wide_inputs * inv_rms * norm_gain).astype(jnp.bfloat16)
-    in_panel, out_panel = (
-        lax.all_gather(in_weight, "seq", axis=0, tiled=True),
-        lax.all_gather(out_weight, "seq", axis=1, tiled=True),
-    )
+    in_half = lax.all_gather(in_weight, "chips", axis=0)
+    in_panel = lax.all_gather(in_half, "core", axis=1).reshape(model_width, 3, slab_width)
+    out_half = lax.all_gather(out_weight, "chips", axis=1)
+    out_panel = lax.all_gather(out_half, "core", axis=2).reshape(slab_width, model_width)
     in_flat = in_panel.reshape(model_width, 3 * slab_width)
     projected = jnp.dot(normed, in_flat, preferred_element_type=jnp.float32)
     projected = projected.astype(jnp.bfloat16).reshape(local_rows, 3, slab_width)
-    upper_rim = passed_along(projected[local_rows - (taps - 1) :], "seq", 1)
+    upper_rim = passed_along(projected[local_rows - (taps - 1) :], SEQ, 1)
     extended = jnp.concatenate([upper_rim, projected], 0).astype(jnp.float32)
     mixed = jnp.zeros((local_rows, 3, slab_width), jnp.float32)
     for offset in range(taps):
@@ -126,7 +128,7 @@
     returned = to_rows(outs)
     conv_out = returned[0]
     back_conv = returned[1]
-    filter_grad = returned[2] * float(local_rows * lax.axis_size("seq")) ** (-0.5)
+    filter_grad = returned[2] * float(local_rows * lax.axis_size(SEQ)) ** (-0.5)
     biased = conv_out + conv_bias * product
     gated = (query_br * biased).astype(jnp.bfloat16)
     partial_out = jnp.dot(gated, out_panel, preferred_element_type=jnp.float32)
@@ -138,7 +140,7 @@
     block_out = (residual + summed).astype(jnp.bfloat16)
     source_grad = back_conv + conv_bias * carried
     mixed_grad = jnp.stack([gate_grad * biased, source_grad * value_br, source_grad * key_br], 1)
-    lower_rim = passed_along(mixed_grad[: taps - 1], "seq", -1)
+    lower_rim = passed_along(mixed_grad[: taps - 1], SEQ, -1)
     extended_back = jnp.concatenate([mixed_grad, lower_rim], 0)
     proj_grad = jnp.zeros((local_rows, 3, slab_width), jnp.float32)
     for offset in range(taps):
@@ -166,19 +168,23 @@
 
 
 def solution(mesh):
+    seq_size, ch_size = mesh.devices.shape
+    split_mesh = jax.sharding.Mesh(
+        mesh.devices.reshape(seq_size // CORES, CORES, ch_size), ("chips", "core", "ch")
+    )
     return jax.shard_map(
         per_device,
-        mesh=mesh,
+        mesh=split_mesh,
         in_specs=(
-            P("seq", None),
+            P(SEQ, None),
             P(),
-            P("seq", None, "ch"),
+            P(SEQ, None, "ch"),
             P(None, None, "ch"),
-            P("seq", "ch"),
+            P(SEQ, "ch"),
             P("ch"),
-            P("ch", "seq"),
-            P("seq", None),
+            P("ch", SEQ),
+            P(SEQ, None),
         ),
-        out_specs=(P("seq", "ch"), P("seq", None), P("seq", "ch")),
+        out_specs=(P(SEQ, "ch"), P(SEQ, None), P(SEQ, "ch")),
         check_vma=False,
     )

time: 340 us -> 383 us (1.13)
  waiting for transfers between devices: 228 us -> 261 us
  local copies, waits for them, and re-layouts: 15.6 us -> 23.5 us
    all_gather x2 -> x4, waiting for transfers between devices: 143 us -> 176 us  [the longest x1 83 us: per_device(): in_half = lax.all_gather(in_weight, 'chips', axis=0)]
    all_gather x1 -> x2, local copies, waits for them, and re-layouts: 8.72 us -> 15.2 us  [the longest x1 9.84 us: per_device(): lax.all_gather(in_half, 'core', axis=1).reshape(model_width, 3, slab_width)]
  transfers between devices with their start and end apart: 8 -> 10, of which waited for: 7 -> 10; matrix products, arithmetic and copies ran while one was open for 7% -> 8% of each run, Pallas kernels for 0% -> 0%
where the time goes in v3:
time: 383 us; the launch traced here: 382 us
  waiting for transfers between devices  261 us (68%)
  matrix products  33.2 us (9%)
  blocking collectives  29 us (8%)
  local copies, waits for them, and re-layouts  23.5 us (6%)
  starting transfers between devices  15.2 us (4%)
  between operations  14.5 us (4%)
  other arithmetic  5.72 us (1%)
    all_gather x1, waiting for transfers between devices, per_device(): in_half = lax.all_gather(in_weight, 'chips', axis=0)  83 us
    all_gather x1, waiting for transfers between devices, per_device(): out_half = lax.all_gather(out_weight, 'chips', axis=1)  70.2 us
    all_gather x1, waiting for transfers between devices, per_device(): in_grad = lax.all_gather(in_grad_share, 'ch', axis=1, tiled=True)  25.8 us
    all_gather x1, waiting for transfers between devices, per_device(): lax.all_gather(in_half, 'core', axis=1).reshape(model_width, 3, slab_width)  22.2 us
    all_to_all x1, blocking collectives, to_rows(): lax.all_to_all(pieces, SEQ, split_axis=0, concat_axis=0, tiled=True)  20.8 us
    reduce_scatter x1, waiting for transfers between devices, per_device(): lax.psum_scatter(partial_grad.astype(jnp.bfloat16), 'ch', scatter_dimensi...  19.8 us
    reduce_scatter x1, waiting for transfers between devices, per_device(): lax.psum_scatter(partial_out.astype(jnp.bfloat16), 'ch', scatter_dimensio...  19.2 us
    all_to_all x1, waiting for transfers between devices, to_columns(): return lax.all_to_all(signals, SEQ, split_axis=1, concat_axis=2, tiled=True)  15.7 us
  transfers between devices with their start and end apart: 10, of which 10 were waited for; matrix products, arithmetic and copies ran while one was open for 8% of the time, Pallas kernels for 0%

profile of v3, /device:TPU:2, one launch (start us, length us, event | category | flops | bytes accessed | tf_op | source)
XLA Modules:
  0.0 382.3 jit_solution(5130750698121017676)
XLA Ops:
  8.7 83.0 %all-gather.12.cloned.1.call-done = bf16[2048,3,256]{2,0,1:T(8,128)(2,1)} async-done(((bf16[64,3,256]{2,0,1:T(8,128)(2,1)}), bf16[2048,3,256]{2,0,1:T(8,128)(2,1)}) %all-gather.12.cloned.1.call-update) | async-done | bytes 3145744 | tf_op jit(solution)/shard_map/all_gather | solution.py:96
  91.7 5.4 %copy.81 = bf16[32,64,3,256]{3,0,2,1:T(8,128)(2,1)} copy(bf16[32,64,3,256]{3,1,0,2:T(8,128)(2,1)} %bitcast.131) | data formatting | bytes 6291456 | tf_op jit(solution)/shard_map/all_gather | solution.py:96
  97.2 70.2 %all-gather.16.cloned.1.call-done = bf16[256,2048]{0,1:T(8,128)(2,1)} async-done(((bf16[256,64]{0,1:T(8,128)(2,1)}), bf16[256,2048]{0,1:T(8,128)(2,1)}) %all-gather.16.cloned.1.call-update) | async-done | bytes 1048592 | tf_op jit(solution)/shard_map/all_gather | solution.py:98
  167.8 22.2 %all-gather.14.cloned.1.call-done = bf16[32,128,3,256]{3,0,2,1:T(8,128)(2,1)} async-done(((bf16[32,64,3,256]{3,0,2,1:T(8,128)(2,1)}), bf16[32,128,3,256]{3,0,2,1:T(8,128)(2,1)}) %all-gather.14.cloned.1.call-update) | async-done | bytes 6291472 | tf_op jit(solution)/shard_map/all_gather | solution.py:97
  190.0 9.8 %copy.82 = bf16[32,128,3,256]{1,0,3,2:T(8,128)(2,1)} copy(bf16[32,128,3,256]{3,0,2,1:T(8,128)(2,1)} %all-gather.14.cloned.1.call-done) | data formatting | bytes 12582912 | tf_op jit(solution)/shard_map/all_gather | solution.py:97
  199.8 6.0 %fusion.11 = bf16[128,768]{1,0:T(8,128)(2,1)S(1)} fusion(bf16[96,8,32,128]{3,2,1,0:T(8,128)(2,1)} %bitcast.125, f32[4096]{0:T(1024)S(1)} %copy-done.8, f32[128]{0:T(128)S(1)} %get-tuple-element.30, bf16[128,4096]{1,0:T(8,128)(2,1)S(1)} %copy-done.1), kind=kOutput, calls=%fused_computation.19 | convolution fusion | flops 807501824 | bytes 7553536 | tf_op jit(solution)/shard_map/dot_general | solution.py:101
  205.8 2.2 collective-permute-start
  208.9 2.0 fusion.152
  211.2 1.6 collective-permute-done
  214.1 9.7 %all-to-all-start = ((f32[3,256,128]{2,0,1:T(4,128)}), f32[3,256,128]{2,0,1:T(4,128)S(1)}, u32[]{:S(2)}, u32[]{:S(2)}) async-start(f32[3,256,128]{2,0,1:T(4,128)} %copy.86), calls=%async_computation | async-start | bytes 1048576 | tf_op jit(solution)/shard_map/all_to_all | solution.py:21
  224.7 15.7 %all-to-all-done = f32[3,256,128]{2,0,1:T(4,128)S(1)} async-done(((f32[3,256,128]{2,0,1:T(4,128)}), f32[3,256,128]{2,0,1:T(4,128)S(1)}, u32[]{:S(2)}, u32[]{:S(2)}) %all-to-all-start) | async-done | bytes 393248 | tf_op jit(solution)/shard_map/all_to_all | solution.py:21
  246.6 1.6 convolution_subtract_fusion.1
  248.3 1.6 convolution_add_fusion.1
  257.3 20.8 %all_to_all.20 = f32[64,3,4,128]{3,2,1,0:T(4,128)S(1)} all-to-all(f32[64,3,4,128]{3,2,1,0:T(4,128)S(1)} %copy.101), channel_id=1, replica_groups=mesh['chips'=32,'core'=2,'ch'=4] {'chips','core'}, dimensions={0} | all-to-all | bytes 786432 | tf_op jit(solution)/shard_map/all_to_all | solution.py:29
  279.1 2.9 collective-permute-start.1
  284.3 6.3 %fusion.6 = bf16[128,4096]{1,0:T(8,128)(2,1)} fusion(bf16[128,768]{0,1:T(8,128)(2,1)} %bitcast.137, bf16[96,8,32,128]{3,2,1,0:T(8,128)(2,1)} %bitcast.126), kind=kOutput, calls=%fused_computation.6 | convolution fusion | flops 805830656 | bytes 7536640 | tf_op jit(solution)/shard_map/dot_general | solution.py:152
  290.7 1.7 copy.102
  292.4 2.7 convolution_convert_fusion
  296.1 19.8 %reduce-scatter.5.cloned.1.call-done = bf16[128,1024]{1,0:T(8,128)(2,1)} async-done(((bf16[128,4096]{1,0:T(8,128)(2,1)}), bf16[128,1024]{1,0:T(8,128)(2,1)}) %reduce-scatter.5.cloned.1.call-update) | async-done | bytes 262160 | tf_op jit(solution)/shard_map/reduce_scatter | solution.py:153
  317.0 8.2 %psum.7 = f32[128,1]{0,1:T(1,128)S(1)} all-reduce(f32[128,1]{0,1:T(1,128)S(1)} %bitcast.144), channel_id=1, replica_groups=mesh['chips'=32,'core'=2,'ch'=4] {'ch'}, use_global_device_ids=true, to_apply=%region_4.5 | all-reduce | flops 128 | bytes 1024 | tf_op jit(solution)/shard_map/psum | solution.py:162
  325.2 19.2 %reduce-scatter.3.cloned.1.call-done = bf16[128,1024]{1,0:T(8,128)(2,1)} async-done(((bf16[128,4096]{1,0:T(8,128)(2,1)}), bf16[128,1024]{1,0:T(8,128)(2,1)}) %reduce-scatter.3.cloned.1.call-update) | async-done | bytes 262160 | tf_op jit(solution)/shard_map/reduce_scatter | solution.py:135
  344.4 2.2 subtract_convert_fusion
  347.3 25.8 %all-gather.10.cloned.1.call-done = bf16[128,4096]{1,0:T(8,128)(2,1)} async-done(((bf16[128,1024]{1,0:T(8,128)(2,1)}), bf16[128,4096]{1,0:T(8,128)(2,1)}) %all-gather.10.cloned.1.call-update) | async-done | bytes 1048592 | tf_op jit(solution)/shard_map/all_gather | solution.py:166
  373.1 2.3 copy.152
  (80 shorter events, 25.0 us)
Async XLA Ops:
  7.2 84.6 %all-gather.12.cloned.1.call-start = ((), (), s32[]{:S(2)}) async-start(), calls=%async_computation.7 | async-start | bytes 3244032 | tf_op jit(solution)/shard_map/all_gather | solution.py:96
  7.9 159.5 %all-gather.16.cloned.1.call-start = ((), (), s32[]{:S(2)}) async-start(), calls=%async_computation.9 | async-start | bytes 1081344 | tf_op jit(solution)/shard_map/all_gather | solution.py:98
  8.6 181.3 %all-gather.14.cloned.1.call-start = ((), (), s32[]{:S(2)}) async-start(), calls=%async_computation.8 | async-start | bytes 9437184 | tf_op jit(solution)/shard_map/all_gather | solution.py:97
  97.1 70.4 %copy-start.6 = (f32[3,3,256]{2,1,0:T(4,128)S(1)}, f32[3,3,256]{2,1,0:T(4,128)}, u32[]{:S(2)}) copy-start(f32[3,3,256]{2,1,0:T(4,128)} %param.11) | copy-start | bytes 27652
  97.1 70.4 %copy-start.1 = (bf16[128,4096]{1,0:T(8,128)(2,1)S(1)}, bf16[128,4096]{1,0:T(8,128)(2,1)}, u32[]{:S(2)}) copy-start(bf16[128,4096]{1,0:T(8,128)(2,1)} %param.8) | copy-start | bytes 3145732
  97.1 111.7 %all-gather.18.cloned.1.call-start = ((), (), s32[]{:S(2)}) async-start(), calls=%async_computation.10 | async-start | bytes 3145728 | tf_op jit(solution)/shard_map/all_gather | solution.py:99
  167.8 32.0 %copy-start.8 = (f32[4096]{0:T(1024)S(1)}, f32[4096]{0:T(1024)}, u32[]{:S(2)}) copy-start(f32[4096]{0:T(1024)} %param.9) | copy-start | bytes 49156
  199.8 9.1 %copy-start.2 = (bf16[128,4096]{1,0:T(8,128)(2,1)S(1)}, bf16[128,4096]{1,0:T(8,128)(2,1)}, u32[]{:S(2)}) copy-start(bf16[128,4096]{1,0:T(8,128)(2,1)} %param.15) | copy-start | bytes 3145732
  205.8 7.0 %collective-permute-start = (bf16[2,3,256]{2,0,1:T(2,128)(2,1)S(1)}, bf16[2,3,256]{2,0,1:T(2,128)(2,1)S(1)}, u32[]{:S(2)}, u32[]{:S(2)}) collective-permute-start(bf16[2,3,256]{2,0,1:T(2,128)(2,1)S(1)} %bitcast.143), channel_id=1, source_target_pairs={{0,4},{4,8},{8,12},{12,16},{16,20},{20,24},{24,28},{28,32},{32,36}... | collective-permute-start | bytes 9224 | tf_op jit(solution)/shard_map/ppermute | solution.py:17
  210.9 2.2 copy-start.5
  214.1 26.3 %all-to-all-start = ((f32[3,256,128]{2,0,1:T(4,128)}), f32[3,256,128]{2,0,1:T(4,128)S(1)}, u32[]{:S(2)}, u32[]{:S(2)}) async-start(f32[3,256,128]{2,0,1:T(4,128)} %copy.86), calls=%async_computation | async-start | bytes 1048576 | tf_op jit(solution)/shard_map/all_to_all | solution.py:21
  223.8 92.2 %reduce-scatter.5.cloned.1.call-start = ((), (), s32[]{:S(2)}) async-start(), calls=%async_computation.5 | async-start | bytes 1310720 | tf_op jit(solution)/shard_map/reduce_scatter | solution.py:153
  255.9 23.1 %copy-start.7 = (f32[256]{0:T(256)S(1)}, f32[256]{0:T(256)}, u32[]{:S(2)}) copy-start(f32[256]{0:T(256)} %param.13) | copy-start | bytes 3076
  278.8 4.7 %copy-start.3 = (f32[1,128,64,4]{1,3,0,2:T(4,128)}, f32[1,128,64,4]{1,3,0,2:T(4,128)S(1)}, u32[]{:S(2)}) copy-start(f32[1,128,64,4]{1,3,0,2:T(4,128)S(1)} %get-tuple-element.25) | copy-start | bytes 393220
  279.1 4.2 %collective-permute-start.1 = (f32[2,3,256]{2,0,1:T(2,128)S(1)}, f32[2,3,256]{2,0,1:T(2,128)S(1)}, u32[]{:S(2)}, u32[]{:S(2)}) collective-permute-start(f32[2,3,256]{2,0,1:T(2,128)S(1)} %slice.113), channel_id=1, source_target_pairs={{4,0},{8,4},{12,8},{16,12},{20,16},{24,20},{28,24},{32,28},{36,32}... | collective-permute-start | bytes 18440 | tf_op jit(solution)/shard_map/ppermute | solution.py:17
  284.3 8.0 %copy-start = (bf16[256,32,128]{0,2,1:T(8,128)(2,1)S(1)}, bf16[256,32,128]{0,2,1:T(8,128)(2,1)}, u32[]{:S(2)}) copy-start(bf16[256,32,128]{0,2,1:T(8,128)(2,1)} %all-gather.18.cloned.1.call-done) | copy-start | bytes 6291460
  290.6 53.7 %reduce-scatter.3.cloned.1.call-start = ((), (), s32[]{:S(2)}) async-start(), calls=%async_computation.4 | async-start | bytes 1310720 | tf_op jit(solution)/shard_map/reduce_scatter | solution.py:135
  295.1 78.0 %all-gather.10.cloned.1.call-start = ((), (), s32[]{:S(2)}) async-start(), calls=%async_computation.6 | async-start | bytes 1310720 | tf_op jit(solution)/shard_map/all_gather | solution.py:166
  295.4 51.2 %copy-start.4 = (f32[1,128,64,4]{1,3,0,2:T(4,128)S(1)}, f32[1,128,64,4]{1,3,0,2:T(4,128)}, u32[]{:S(2)}) copy-start(f32[1,128,64,4]{1,3,0,2:T(4,128)} %get-tuple-element.23) | copy-start | bytes 393220
Sparse Core Ops, SparseCore 0:
  10.6 81.1 all-gather.11
  94.3 73.0 all-gather.15
  169.2 20.7 all-gather.13
  191.6 17.1 all-gather.17
  290.8 25.1 reduce-scatter.4
  318.3 25.9 reduce-scatter.2
  346.7 26.3 all-gather.9

commit v4 on v2

--- a/solution.py
+++ b/solution.py
@@ -13,6 +13,21 @@
     devices = range(lax.axis_size(axis))
     route = [(i - distance, i) for i in devices if i - distance in devices]
     return lax.ppermute(block, axis, route)
+
+
+def doubled_gather(block, axis):
+    devices = lax.axis_size(axis)
+    place = lax.axis_index(axis)
+    bits = devices.bit_length() - 1
+    assert 1 << bits == devices
+    gathered = block
+    for bit in reversed(range(bits)):
+        route = [(i, i ^ (1 << bit)) for i in range(devices)]
+        arrived = lax.ppermute(gathered, axis, route)
+        lower = ((place >> bit) & 1) == 0
+        gathered = jnp.where(lower, jnp.stack([gathered, arrived]), jnp.stack([arrived, gathered]))
+    gathered = gathered.transpose(tuple(reversed(range(bits))) + tuple(range(bits, gathered.ndim)))
+    return gathered.reshape((devices * block.shape[0],) + block.shape[1:])
 
 
 def to_columns(signals):
@@ -93,7 +108,7 @@
     normed = (wide_inputs * inv_rms * norm_gain).astype(jnp.bfloat16)
     in_panel, out_panel = (
         lax.all_gather(in_weight, "seq", axis=0, tiled=True),
-        lax.all_gather(out_weight, "seq", axis=1, tiled=True),
+        doubled_gather(out_weight.T, "seq").T,
     )
     in_flat = in_panel.reshape(model_width, 3 * slab_width)
     projected = jnp.dot(normed, in_flat, preferred_element_type=jnp.float32)

time: 340 us -> 291 us (0.86)
  waiting for transfers between devices: 228 us -> 151 us
  starting transfers between devices: 13.2 us -> 25.4 us
  local copies, waits for them, and re-layouts: 15.6 us -> 23.8 us
  other arithmetic: 7.48 us -> 12.7 us
    all_gather x1 -> x0, waiting for transfers between devices: 61.2 us -> none  [per_device(): lax.all_gather(out_weight, 'seq', axis=1, tiled=True)]
    all_gather x1, waiting for transfers between devices: 82 us -> 32.6 us  [per_device(): lax.all_gather(in_weight, 'seq', axis=0, tiled=True)]
    ppermute x0 -> x6, waiting for transfers between devices: none -> 36.6 us  [doubled_gather(): arrived = lax.ppermute(gathered, axis, route)]
    ppermute x0 -> x6, starting transfers between devices: none -> 13.6 us  [doubled_gather(): arrived = lax.ppermute(gathered, axis, route)]
    all_to_all x1, waiting for transfers between devices: 15.7 us -> 11.4 us  [to_columns(): lax.all_to_all(signals, 'seq', split_axis=1, concat_axis=2, tiled=True)]
    ppermute x2, waiting for transfers between devices: 1.33 us -> 4.93 us  [passed_along(): return lax.ppermute(block, axis, route)]
  transfers between devices with their start and end apart: 8 -> 13, of which waited for: 7 -> 13; matrix products, arithmetic and copies ran while one was open for 7% -> 6% of each run, Pallas kernels for 0% -> 0%
where the time goes in v4:
time: 291 us; the launch traced here: 290 us
  waiting for transfers between devices  151 us (52%)
  matrix products  33.1 us (11%)
  blocking collectives  29 us (10%)
  starting transfers between devices  25.4 us (9%)
  local copies, waits for them, and re-layouts  23.8 us (8%)
  between operations  14.2 us (5%)
  other arithmetic  12.7 us (4%)
    ppermute x6, waiting for transfers between devices, doubled_gather(): arrived = lax.ppermute(gathered, axis, route)  36.6 us
    all_gather x1, waiting for transfers between devices, per_device(): lax.all_gather(in_weight, 'seq', axis=0, tiled=True)  32.6 us
    all_gather x1, waiting for transfers between devices, per_device(): in_grad = lax.all_gather(in_grad_share, 'ch', axis=1, tiled=True)  25.9 us
    all_to_all x1, blocking collectives, to_rows(): lax.all_to_all(pieces, 'seq', split_axis=0, concat_axis=0, tiled=True)  20.8 us
    reduce_scatter x1, waiting for transfers between devices, per_device(): lax.psum_scatter(partial_grad.astype(jnp.bfloat16), 'ch', scatter_dimensi...  19.8 us
    reduce_scatter x1, waiting for transfers between devices, per_device(): lax.psum_scatter(partial_out.astype(jnp.bfloat16), 'ch', scatter_dimensio...  19.3 us
    ppermute x6, starting transfers between devices, doubled_gather(): arrived = lax.ppermute(gathered, axis, route)  13.6 us
    all_to_all x1, waiting for transfers between devices, to_columns(): lax.all_to_all(signals, 'seq', split_axis=1, concat_axis=2, tiled=True)  11.4 us
  transfers between devices with their start and end apart: 13, of which 13 were waited for; matrix products, arithmetic and copies ran while one was open for 6% of the time, Pallas kernels for 0%

profile of v4, /device:TPU:2, one launch (start us, length us, event | category | flops | bytes accessed | tf_op | source)
XLA Modules:
  0.0 289.6 jit_solution(6743141574618619584)
XLA Ops:
  7.9 2.2 collective-permute-start.1
  10.1 3.5 %collective-permute-done.1 = bf16[64,256]{1,0:T(8,128)(2,1)S(1)} collective-permute-done((bf16[64,256]{1,0:T(8,128)(2,1)}, bf16[64,256]{1,0:T(8,128)(2,1)S(1)}, u32[]{:S(2)}, u32[]{:S(2)}) %collective-permute-start.1) | collective-permute-done | bytes 32800 | tf_op jit(solution)/shard_map/ppermute | solution.py:26
  14.5 2.3 collective-permute-start.2
  19.1 7.1 %collective-permute-start.3 = (bf16[2,2,64,256]{3,2,0,1:T(8,128)(2,1)S(1)}, bf16[2,2,64,256]{3,2,0,1:T(8,128)(2,1)S(1)}, u32[]{:S(2)}, u32[]{:S(2)}) collective-permute-start(bf16[2,2,64,256]{3,2,0,1:T(8,128)(2,1)S(1)} %maximum_select_fusion.4), channel_id=1, source_target_pairs={{0,32},{4,36},{8,40},{12,44},{16,48},{20,52},{24,56},{28,60},{32,0... | collective-permute-start | bytes 393224 | tf_op jit(solution)/shard_map/ppermute | solution.py:26
  26.2 4.4 %collective-permute-done.3 = bf16[2,2,64,256]{3,2,0,1:T(8,128)(2,1)S(1)} collective-permute-done((bf16[2,2,64,256]{3,2,0,1:T(8,128)(2,1)S(1)}, bf16[2,2,64,256]{3,2,0,1:T(8,128)(2,1)S(1)}, u32[]{:S(2)}, u32[]{:S(2)}) %collective-permute-start.3) | collective-permute-done | bytes 131104 | tf_op jit(solution)/shard_map/ppermute | solution.py:26
  32.5 12.3 %collective-permute-done.4 = bf16[2,2,2,64,256]{4,3,0,1,2:T(8,128)(2,1)S(1)} collective-permute-done((bf16[2,2,2,64,256]{4,3,0,1,2:T(8,128)(2,1)S(1)}, bf16[2,2,2,64,256]{4,3,0,1,2:T(8,128)(2,1)S(1)}, u32[]{:S(2)}, u32[]{:S(2)}) %collective-permute-start.4) | collective-permute-done | bytes 262176 | tf_op jit(solution)/shard_map/ppermute | solution.py:26
  45.2 14.3 %collective-permute-done.5 = bf16[2,2,2,2,64,256]{5,4,0,1,2,3:T(8,128)(2,1)S(1)} collective-permute-done((bf16[2,2,2,2,64,256]{5,4,0,1,2,3:T(8,128)(2,1)S(1)}, bf16[2,2,2,2,64,256]{5,4,0,1,2,3:T(8,128)(2,1)S(1)}, u32[]{:S(2)}, u32[]{:S(2)}) %collective-permute-start.5) | collective-permute-done | bytes 524320 | tf_op jit(solution)/shard_map/ppermute | solution.py:26
  62.6 32.6 %all-gather.3.cloned.1.call-done = bf16[4096,3,256]{2,0,1:T(8,128)(2,1)} async-done(((bf16[64,3,256]{2,0,1:T(8,128)(2,1)}), bf16[4096,3,256]{2,0,1:T(8,128)(2,1)}) %all-gather.3.cloned.1.call-update) | async-done | bytes 6291472 | tf_op jit(solution)/shard_map/all_gather | solution.py:110
  95.2 8.7 %copy.65 = bf16[4096,3,256]{0,2,1:T(8,128)(2,1)} copy(bf16[4096,3,256]{2,0,1:T(8,128)(2,1)} %all-gather.3.cloned.1.call-done) | data formatting | bytes 12582912 | tf_op jit(solution)/shard_map/all_gather | solution.py:110
  103.9 5.1 %convolution_convert_fusion.1 = bf16[128,768]{1,0:T(8,128)(2,1)S(1)} fusion(bf16[4096,768]{0,1:T(8,128)(2,1)} %bitcast.154, f32[4096]{0:T(1024)S(1)} %copy-done.9, f32[128]{0:T(128)S(1)} %get-tuple-element.35, bf16[128,4096]{1,0:T(8,128)(2,1)S(1)} %copy-done), kind=kOutput, calls=%fused_computation.15 | convolution fusion | flops 807501824 | bytes 7553536 | tf_op jit(solution)/shard_map/dot_general | solution.py:114
  113.2 3.6 %collective-permute-done = bf16[2,3,256]{2,0,1:T(2,128)(2,1)S(1)} collective-permute-done((bf16[2,3,256]{2,0,1:T(2,128)(2,1)}, bf16[2,3,256]{2,0,1:T(2,128)(2,1)S(1)}, u32[]{:S(2)}, u32[]{:S(2)}) %collective-permute-start) | collective-permute-done | bytes 3104 | tf_op jit(solution)/shard_map/ppermute | solution.py:15
  119.9 6.4 %all-to-all-start = ((f32[3,256,128]{2,0,1:T(4,128)}), f32[3,256,128]{2,0,1:T(4,128)}, u32[]{:S(2)}, u32[]{:S(2)}) async-start(f32[3,256,128]{2,0,1:T(4,128)} %copy.79), calls=%async_computation | async-start | bytes 1048576 | tf_op jit(solution)/shard_map/all_to_all | solution.py:34
  131.5 11.4 %all-to-all-done = f32[3,256,128]{2,0,1:T(4,128)} async-done(((f32[3,256,128]{2,0,1:T(4,128)}), f32[3,256,128]{2,0,1:T(4,128)}, u32[]{:S(2)}, u32[]{:S(2)}) %all-to-all-start) | async-done | bytes 393248 | tf_op jit(solution)/shard_map/all_to_all | solution.py:34
  142.9 2.6 convolution_bitcast_fusion.1
  145.5 2.5 fusion.1
  161.9 20.8 %all_to_all.20 = f32[64,3,4,128]{3,2,1,0:T(4,128)S(1)} all-to-all(f32[64,3,4,128]{3,2,1,0:T(4,128)S(1)} %copy.94), channel_id=1, replica_groups=mesh['seq'=64,'ch'=4] {'seq'}, dimensions={0} | all-to-all | bytes 786432 | tf_op jit(solution)/shard_map/all_to_all | solution.py:42
  187.9 2.9 collective-permute-start.7
  192.2 5.9 %fusion = bf16[128,4096]{1,0:T(8,128)(2,1)} fusion(bf16[4096,3,256]{2,0,1:T(8,128)(2,1)} %all-gather.3.cloned.1.call-done, f32[130,3,256]{2,0,1:T(8,128)S(1)} %pad_maximum_fusion.10, f32[3,256]{1,0:T(4,128)S(1)} %get-tuple-element.36, f32[3,256]{1,0:T(4,128)S(1)} %get-tuple-element.37, f32[3,256]{1,0:T(4,128)S(1)} %bitcast.181, ...), kind=kOutput, calls=%fused_computation.1 | convolution fusion | flops 806617088 | bytes 8531968 | tf_op jit(solution)/shard_map/dot_general | solution.py:165
  199.8 2.7 convolution_convert_fusion
  203.5 19.8 %reduce-scatter.5.cloned.1.call-done = bf16[128,1024]{1,0:T(8,128)(2,1)} async-done(((bf16[128,4096]{1,0:T(8,128)(2,1)}), bf16[128,1024]{1,0:T(8,128)(2,1)}) %reduce-scatter.5.cloned.1.call-update) | async-done | bytes 262160 | tf_op jit(solution)/shard_map/reduce_scatter | solution.py:166
  224.4 8.2 %psum.7 = f32[128,1]{0,1:T(1,128)S(1)} all-reduce(f32[128,1]{0,1:T(1,128)S(1)} %bitcast.183), channel_id=1, replica_groups=mesh['seq'=64,'ch'=4] {'ch'}, use_global_device_ids=true, to_apply=%region_4.5 | all-reduce | flops 128 | bytes 1024 | tf_op jit(solution)/shard_map/psum | solution.py:175
  232.6 19.3 %reduce-scatter.3.cloned.1.call-done = bf16[128,1024]{1,0:T(8,128)(2,1)} async-done(((bf16[128,4096]{1,0:T(8,128)(2,1)}), bf16[128,1024]{1,0:T(8,128)(2,1)}) %reduce-scatter.3.cloned.1.call-update) | async-done | bytes 262160 | tf_op jit(solution)/shard_map/reduce_scatter | solution.py:148
  254.9 25.9 %all-gather.5.cloned.1.call-done = bf16[128,4096]{1,0:T(8,128)(2,1)} async-done(((bf16[128,1024]{1,0:T(8,128)(2,1)}), bf16[128,4096]{1,0:T(8,128)(2,1)}) %all-gather.5.cloned.1.call-update) | async-done | bytes 1048592 | tf_op jit(solution)/shard_map/all_gather | solution.py:179
  280.8 2.3 copy.139
  (104 shorter events, 48.5 us)
Async XLA Ops:
  7.2 88.0 %all-gather.3.cloned.1.call-start = ((), (), s32[]{:S(2)}) async-start(), calls=%async_computation.4 | async-start | bytes 6389760 | tf_op jit(solution)/shard_map/all_gather | solution.py:110
  7.9 5.7 %collective-permute-start.1 = (bf16[64,256]{1,0:T(8,128)(2,1)}, bf16[64,256]{1,0:T(8,128)(2,1)S(1)}, u32[]{:S(2)}, u32[]{:S(2)}) collective-permute-start(bf16[64,256]{1,0:T(8,128)(2,1)} %bitcast.171), channel_id=1, source_target_pairs={{0,128},{4,132},{8,136},{12,140},{16,144},{20,148},{24,152},{28,15... | collective-permute-start | bytes 98312 | tf_op jit(solution)/shard_map/ppermute | solution.py:26
  14.5 4.6 %collective-permute-start.2 = (bf16[2,64,256]{2,1,0:T(8,128)(2,1)S(1)}, bf16[2,64,256]{2,1,0:T(8,128)(2,1)S(1)}, u32[]{:S(2)}, u32[]{:S(2)}) collective-permute-start(bf16[2,64,256]{2,1,0:T(8,128)(2,1)S(1)} %maximum_select_fusion.5), channel_id=1, source_target_pairs={{0,64},{4,68},{8,72},{12,76},{16,80},{20,84},{24,88},{28,92},{32,9... | collective-permute-start | bytes 196616 | tf_op jit(solution)/shard_map/ppermute | solution.py:26
  19.0 26.0 %copy-start.7 = (f32[3,3,256]{2,1,0:T(4,128)S(1)}, f32[3,3,256]{2,1,0:T(4,128)}, u32[]{:S(2)}) copy-start(f32[3,3,256]{2,1,0:T(4,128)} %param.11) | copy-start | bytes 27652
  19.1 11.5 %collective-permute-start.3 = (bf16[2,2,64,256]{3,2,0,1:T(8,128)(2,1)S(1)}, bf16[2,2,64,256]{3,2,0,1:T(8,128)(2,1)S(1)}, u32[]{:S(2)}, u32[]{:S(2)}) collective-permute-start(bf16[2,2,64,256]{3,2,0,1:T(8,128)(2,1)S(1)} %maximum_select_fusion.4), channel_id=1, source_target_pairs={{0,32},{4,36},{8,40},{12,44},{16,48},{20,52},{24,56},{28,60},{32,0... | collective-permute-start | bytes 393224 | tf_op jit(solution)/shard_map/ppermute | solution.py:26
  30.6 14.2 %collective-permute-start.4 = (bf16[2,2,2,64,256]{4,3,0,1,2:T(8,128)(2,1)S(1)}, bf16[2,2,2,64,256]{4,3,0,1,2:T(8,128)(2,1)S(1)}, u32[]{:S(2)}, u32[]{:S(2)}) collective-permute-start(bf16[2,2,2,64,256]{4,3,0,1,2:T(8,128)(2,1)S(1)} %maximum_select_fusion.3), channel_id=1, source_target_pairs={{0,16},{4,20},{8,24},{12,28},{16,0},{20,4},{24,8},{28,12},{32,48},... | collective-permute-start | bytes 786440 | tf_op jit(solution)/shard_map/ppermute | solution.py:26
  44.9 14.6 %collective-permute-start.5 = (bf16[2,2,2,2,64,256]{5,4,0,1,2,3:T(8,128)(2,1)S(1)}, bf16[2,2,2,2,64,256]{5,4,0,1,2,3:T(8,128)(2,1)S(1)}, u32[]{:S(2)}, u32[]{:S(2)}) collective-permute-start(bf16[2,2,2,2,64,256]{5,4,0,1,2,3:T(8,128)(2,1)S(1)} %maximum_select_fusion.2), channel_id=1, source_target_pairs={{0,8},{4,12},{8,0},{12,4},{16,24},{20,28},{24,16},{28,20},{32,40},... | collective-permute-start | bytes 1572872 | tf_op jit(solution)/shard_map/ppermute | solution.py:26
  45.1 14.6 %copy-start = (bf16[128,4096]{1,0:T(8,128)(2,1)S(1)}, bf16[128,4096]{1,0:T(8,128)(2,1)}, u32[]{:S(2)}) copy-start(bf16[128,4096]{1,0:T(8,128)(2,1)} %param.8) | copy-start | bytes 3145732
  59.6 2.7 collective-permute-start.6
  60.5 43.4 %copy-start.11 = (f32[128]{0:T(128)}, f32[128]{0:T(128)S(1)}, u32[]{:S(2)}) copy-start(f32[128]{0:T(128)S(1)} %get-tuple-element.35) | copy-start | bytes 1540
  62.6 41.4 %copy-start.9 = (f32[4096]{0:T(1024)S(1)}, f32[4096]{0:T(1024)}, u32[]{:S(2)}) copy-start(f32[4096]{0:T(1024)} %param.9) | copy-start | bytes 49156
  103.9 7.8 %copy-start.3 = (bf16[128,4096]{1,0:T(8,128)(2,1)S(1)}, bf16[128,4096]{1,0:T(8,128)(2,1)}, u32[]{:S(2)}) copy-start(bf16[128,4096]{1,0:T(8,128)(2,1)} %param.15) | copy-start | bytes 3145732
  109.6 7.2 %collective-permute-start = (bf16[2,3,256]{2,0,1:T(2,128)(2,1)}, bf16[2,3,256]{2,0,1:T(2,128)(2,1)S(1)}, u32[]{:S(2)}, u32[]{:S(2)}) collective-permute-start(bf16[2,3,256]{2,0,1:T(2,128)(2,1)} %bitcast.1), channel_id=1, source_target_pairs={{0,4},{4,8},{8,12},{12,16},{16,20},{20,24},{24,28},{28,32},{32,36}... | collective-permute-start | bytes 9224 | tf_op jit(solution)/shard_map/ppermute | solution.py:15
  119.9 23.0 %all-to-all-start = ((f32[3,256,128]{2,0,1:T(4,128)}), f32[3,256,128]{2,0,1:T(4,128)}, u32[]{:S(2)}, u32[]{:S(2)}) async-start(f32[3,256,128]{2,0,1:T(4,128)} %copy.79), calls=%async_computation | async-start | bytes 1048576 | tf_op jit(solution)/shard_map/all_to_all | solution.py:34
  126.3 97.0 %reduce-scatter.5.cloned.1.call-start = ((), (), s32[]{:S(2)}) async-start(), calls=%async_computation.6 | async-start | bytes 1310720 | tf_op jit(solution)/shard_map/reduce_scatter | solution.py:166
  142.9 5.1 %copy-start.1 = (f32[128,128]{0,1:T(8,128)S(1)}, f32[128,128]{0,1:T(8,128)}, u32[]{:S(2)}) copy-start(f32[128,128]{0,1:T(8,128)} %copy.83) | copy-start | bytes 196612
  142.9 5.1 %copy-start.2 = (f32[128,128]{0,1:T(8,128)S(1)}, f32[128,128]{0,1:T(8,128)}, u32[]{:S(2)}) copy-start(f32[128,128]{0,1:T(8,128)} %copy.82) | copy-start | bytes 196612
  160.5 26.3 %copy-start.8 = (f32[256]{0:T(256)S(1)}, f32[256]{0:T(256)}, u32[]{:S(2)}) copy-start(f32[256]{0:T(256)} %param.13) | copy-start | bytes 3076
  187.9 4.2 %collective-permute-start.7 = (f32[2,3,256]{2,0,1:T(2,128)S(1)}, f32[2,3,256]{2,0,1:T(2,128)S(1)}, u32[]{:S(2)}, u32[]{:S(2)}) collective-permute-start(f32[2,3,256]{2,0,1:T(2,128)S(1)} %slice.113), channel_id=1, source_target_pairs={{4,0},{8,4},{12,8},{16,12},{20,16},{24,20},{28,24},{32,28},{36,32}... | collective-permute-start | bytes 18440 | tf_op jit(solution)/shard_map/ppermute | solution.py:15
  198.1 53.8 %reduce-scatter.3.cloned.1.call-start = ((), (), s32[]{:S(2)}) async-start(), calls=%async_computation.5 | async-start | bytes 1310720 | tf_op jit(solution)/shard_map/reduce_scatter | solution.py:148
  202.5 49.4 %copy-start.10 = (f32[128]{0:T(128)S(1)}, f32[128]{0:T(128)}, u32[]{:S(2)}) copy-start(f32[128]{0:T(128)} %get-tuple-element.34) | copy-start | bytes 1540
  202.5 49.4 %copy-start.12 = (f32[128]{0:T(128)S(1)}, f32[128]{0:T(128)}, u32[]{:S(2)}) copy-start(f32[128]{0:T(128)} %copy-done.11) | copy-start | bytes 1540
  202.5 78.2 %all-gather.5.cloned.1.call-start = ((), (), s32[]{:S(2)}) async-start(), calls=%async_computation.7 | async-start | bytes 1310720 | tf_op jit(solution)/shard_map/all_gather | solution.py:179
  202.8 51.3 %copy-start.5 = (f32[1,128,64,4]{1,3,0,2:T(4,128)S(1)}, f32[1,128,64,4]{1,3,0,2:T(4,128)}, u32[]{:S(2)}) copy-start(f32[1,128,64,4]{1,3,0,2:T(4,128)} %get-tuple-element.24) | copy-start | bytes 393220
  (2 other events, 7.7 us)
Sparse Core Ops, SparseCore 0:
  10.8 84.3 all-gather.2
  198.2 25.0 reduce-scatter.4
  225.9 25.9 reduce-scatter.2
  254.2 26.4 all-gather.4

commit v5 on v4

--- a/solution.py
+++ b/solution.py
@@ -28,6 +28,25 @@
         gathered = jnp.where(lower, jnp.stack([gathered, arrived]), jnp.stack([arrived, gathered]))
     gathered = gathered.transpose(tuple(reversed(range(bits))) + tuple(range(bits, gathered.ndim)))
     return gathered.reshape((devices * block.shape[0],) + block.shape[1:])
+
+
+def halved_sum(partial, axis):
+    devices = lax.axis_size(axis)
+    place = lax.axis_index(axis)
+    bits = devices.bit_length() - 1
+    assert 1 << bits == devices
+    rows, width = partial.shape
+    share = width // devices
+    held = partial.reshape((rows,) + (2,) * bits + (share,))
+    held = held.astype(jnp.float32)
+    for bit in reversed(range(bits)):
+        route = [(i, i ^ (1 << bit)) for i in range(devices)]
+        mine = (place >> bit) & 1
+        kept = lax.dynamic_index_in_dim(held, mine, 1, keepdims=False)
+        given = lax.dynamic_index_in_dim(held, 1 - mine, 1, keepdims=False)
+        arrived = lax.ppermute(given.astype(jnp.bfloat16), axis, route)
+        held = kept + arrived.astype(jnp.float32)
+    return held
 
 
 def to_columns(signals):
@@ -145,9 +164,7 @@
     biased = conv_out + conv_bias * product
     gated = (query_br * biased).astype(jnp.bfloat16)
     partial_out = jnp.dot(gated, out_panel, preferred_element_type=jnp.float32)
-    summed = lax.psum_scatter(
-        partial_out.astype(jnp.bfloat16), "ch", scatter_dimension=1, tiled=True
-    ).astype(jnp.float32)
+    summed = halved_sum(partial_out.astype(jnp.bfloat16), "ch")
     share = summed.shape[1]
     residual = lax.dynamic_slice_in_dim(wide_inputs, lax.axis_index("ch") * share, share, 1)
     block_out = (residual + summed).astype(jnp.bfloat16)
@@ -163,16 +180,29 @@
         )
     proj_grad = proj_grad.astype(jnp.bfloat16).reshape(local_rows, 3 * slab_width)
     partial_grad = jnp.dot(proj_grad, in_flat.T, preferred_element_type=jnp.float32)
-    norm_grad = lax.psum_scatter(
-        partial_grad.astype(jnp.bfloat16), "ch", scatter_dimension=1, tiled=True
-    ).astype(jnp.float32)
-    feature_share = norm_grad.shape[1]
+    ch_size = lax.axis_size("ch")
+    feature_share = model_width // ch_size
+    partial_inner = jnp.sum(partial_grad * (norm_gain * wide_inputs), axis=1, keepdims=True)
+    inner_high = partial_inner.astype(jnp.bfloat16)
+    inner_low = (partial_inner - inner_high.astype(jnp.float32)).astype(jnp.bfloat16)
+    extra = jnp.concatenate(
+        [inner_high, inner_low, jnp.zeros((local_rows, 126), jnp.bfloat16)], axis=1
+    )
+    payload = jnp.concatenate(
+        [
+            partial_grad.astype(jnp.bfloat16).reshape(local_rows, ch_size, feature_share),
+            jnp.broadcast_to(extra[:, None, :], (local_rows, ch_size, 128)),
+        ],
+        axis=2,
+    ).reshape(local_rows, ch_size * (feature_share + 128))
+    reduced = lax.psum_scatter(payload, "ch", scatter_dimension=1, tiled=True).astype(jnp.float32)
+    norm_grad = reduced[:, :feature_share]
+    inner_term = (reduced[:, feature_share : feature_share + 1] + reduced[:, feature_share + 1 : feature_share + 2]) / model_width
     feature_begin = lax.axis_index("ch") * feature_share
     gain_share = lax.dynamic_slice_in_dim(norm_gain, feature_begin, feature_share, 0)
     inputs_share = lax.dynamic_slice_in_dim(wide_inputs, feature_begin, feature_share, 1)
     grad_share = lax.dynamic_slice_in_dim(out_grad, feature_begin, feature_share, 1)
     weighted = norm_grad * gain_share
-    inner_term = lax.psum(jnp.sum(weighted * inputs_share, axis=1, keepdims=True), "ch") / model_width
     in_grad_share = (
         grad_share.astype(jnp.float32) + weighted * inv_rms - inputs_share * inv_rms**3 * inner_term
     ).astype(jnp.bfloat16)

time: 291 us -> 291 us (level)
  waiting for transfers between devices: 151 us -> 136 us
  local copies, waits for them, and re-layouts: 23.8 us -> 38.7 us
  blocking collectives: 29 us -> 20.8 us
  other arithmetic: 12.7 us -> 17.9 us
  starting transfers between devices: 25.4 us -> 28.9 us
    reduce_scatter x2 -> x0, waiting for transfers between devices: 39.1 us -> none  [the longest x1 19.8 us: per_device(): lax.psum_scatter(partial_grad.astype(jnp.bfloat16), 'ch', scatter_dimensi...]
    ppermute x0 -> x2, waiting for transfers between devices: none -> 27.6 us  [halved_sum(): arrived = lax.ppermute(given.astype(jnp.bfloat16), axis, route)]
    psum x1 -> x0, blocking collectives: 8.2 us -> none  [per_device(): lax.psum(jnp.sum(weighted * inputs_share, axis=1, keepdims=True), 'ch')]
    unnamed x30 -> x39, local copies, waits for them, and re-layouts: 3.11 us -> 8.8 us
    convert_element_type x0 -> x4, local copies, waits for them, and re-layouts: none -> 5.35 us  [the longest x1 3.03 us: halved_sum(): held = held.astype(jnp.float32)]
    concatenate x0 -> x2, other arithmetic: none -> 3.69 us  [the longest x1 2.83 us: per_device(): jnp.concatenate([partial_grad.astype(jnp.bfloat16).reshape(local_rows, ch...]
    ppermute x0 -> x2, starting transfers between devices: none -> 3.65 us  [halved_sum(): arrived = lax.ppermute(given.astype(jnp.bfloat16), axis, route)]
  transfers between devices with their start and end apart: 13 -> 14, of which waited for: 13 -> 13; matrix products, arithmetic and copies ran while one was open for 6% -> 9% of each run, Pallas kernels for 0% -> 0%
where the time goes in v5:
time: 291 us; the launch traced here: 290 us
  waiting for transfers between devices  136 us (47%)
  local copies, waits for them, and re-layouts  38.7 us (13%)
  matrix products  33.6 us (12%)
  starting transfers between devices  28.9 us (10%)
  blocking collectives  20.8 us (7%)
  other arithmetic  17.9 us (6%)
  between operations  14.3 us (5%)
    ppermute x6, waiting for transfers between devices, doubled_gather(): arrived = lax.ppermute(gathered, axis, route)  36.5 us
    all_gather x1, waiting for transfers between devices, per_device(): lax.all_gather(in_weight, 'seq', axis=0, tiled=True)  32 us
    ppermute x2, waiting for transfers between devices, halved_sum(): arrived = lax.ppermute(given.astype(jnp.bfloat16), axis, route)  27.6 us
    all_gather x1, waiting for transfers between devices, per_device(): in_grad = lax.all_gather(in_grad_share, 'ch', axis=1, tiled=True)  23.2 us
    all_to_all x1, blocking collectives, to_rows(): lax.all_to_all(pieces, 'seq', split_axis=0, concat_axis=0, tiled=True)  20.8 us
    ppermute x6, starting transfers between devices, doubled_gather(): arrived = lax.ppermute(gathered, axis, route)  13.5 us
    all_to_all x1, waiting for transfers between devices, to_columns(): lax.all_to_all(signals, 'seq', split_axis=1, concat_axis=2, tiled=True)  11.4 us
    unnamed x39, local copies, waits for them, and re-layouts  8.8 us
  transfers between devices with their start and end apart: 14, of which 13 were waited for; matrix products, arithmetic and copies ran while one was open for 9% of the time, Pallas kernels for 0%

profile of v5, /device:TPU:2, one launch (start us, length us, event | category | flops | bytes accessed | tf_op | source)
XLA Modules:
  0.0 289.8 jit_solution(16058545294507999682)
XLA Ops:
  10.1 3.5 %collective-permute-done.1 = bf16[64,256]{1,0:T(8,128)(2,1)S(1)} collective-permute-done((bf16[64,256]{1,0:T(8,128)(2,1)}, bf16[64,256]{1,0:T(8,128)(2,1)S(1)}, u32[]{:S(2)}, u32[]{:S(2)}) %collective-permute-start.1) | collective-permute-done | bytes 32800 | tf_op jit(solution)/shard_map/ppermute | solution.py:26
  19.1 7.1 %collective-permute-start.3 = (bf16[2,2,64,256]{3,2,0,1:T(8,128)(2,1)S(1)}, bf16[2,2,64,256]{3,2,0,1:T(8,128)(2,1)S(1)}, u32[]{:S(2)}, u32[]{:S(2)}) collective-permute-start(bf16[2,2,64,256]{3,2,0,1:T(8,128)(2,1)S(1)} %maximum_select_fusion.4), channel_id=1, source_target_pairs={{0,32},{4,36},{8,40},{12,44},{16,48},{20,52},{24,56},{28,60},{32,0... | collective-permute-start | bytes 393224 | tf_op jit(solution)/shard_map/ppermute | solution.py:26
  26.2 4.4 %collective-permute-done.3 = bf16[2,2,64,256]{3,2,0,1:T(8,128)(2,1)S(1)} collective-permute-done((bf16[2,2,64,256]{3,2,0,1:T(8,128)(2,1)S(1)}, bf16[2,2,64,256]{3,2,0,1:T(8,128)(2,1)S(1)}, u32[]{:S(2)}, u32[]{:S(2)}) %collective-permute-start.3) | collective-permute-done | bytes 131104 | tf_op jit(solution)/shard_map/ppermute | solution.py:26
  32.5 12.3 %collective-permute-done.4 = bf16[2,2,2,64,256]{4,3,0,1,2:T(8,128)(2,1)S(1)} collective-permute-done((bf16[2,2,2,64,256]{4,3,0,1,2:T(8,128)(2,1)S(1)}, bf16[2,2,2,64,256]{4,3,0,1,2:T(8,128)(2,1)S(1)}, u32[]{:S(2)}, u32[]{:S(2)}) %collective-permute-start.4) | collective-permute-done | bytes 262176 | tf_op jit(solution)/shard_map/ppermute | solution.py:26
  45.9 14.3 %collective-permute-done.5 = bf16[2,2,2,2,64,256]{5,4,0,1,2,3:T(8,128)(2,1)S(1)} collective-permute-done((bf16[2,2,2,2,64,256]{5,4,0,1,2,3:T(8,128)(2,1)}, bf16[2,2,2,2,64,256]{5,4,0,1,2,3:T(8,128)(2,1)S(1)}, u32[]{:S(2)}, u32[]{:S(2)}) %collective-permute-start.5) | collective-permute-done | bytes 524320 | tf_op jit(solution)/shard_map/ppermute | solution.py:26
  63.2 32.0 %all-gather.3.cloned.1.call-done = bf16[4096,3,256]{2,0,1:T(8,128)(2,1)} async-done(((bf16[64,3,256]{2,0,1:T(8,128)(2,1)}), bf16[4096,3,256]{2,0,1:T(8,128)(2,1)}) %all-gather.3.cloned.1.call-update) | async-done | bytes 6291472 | tf_op jit(solution)/shard_map/all_gather | solution.py:129
  95.2 8.7 %copy.73 = bf16[4096,3,256]{0,2,1:T(8,128)(2,1)} copy(bf16[4096,3,256]{2,0,1:T(8,128)(2,1)} %all-gather.3.cloned.1.call-done) | data formatting | bytes 12582912 | tf_op jit(solution)/shard_map/all_gather | solution.py:129
  103.9 5.1 %convolution_convert_fusion.1 = bf16[128,768]{1,0:T(8,128)(2,1)S(1)} fusion(bf16[4096,768]{0,1:T(8,128)(2,1)} %bitcast.173, bf16[128,4096]{1,0:T(8,128)(2,1)S(1)} %copy-done, f32[4096]{0:T(1024)S(1)} %copy-done.10, f32[128]{0:T(128)S(1)} %get-tuple-element.37), kind=kOutput, calls=%fused_computation.17 | convolution fusion | flops 807501824 | bytes 7553536 | tf_op jit(solution)/shard_map/dot_general | solution.py:133
  113.2 3.6 %collective-permute-done = bf16[2,3,256]{2,0,1:T(2,128)(2,1)S(1)} collective-permute-done((bf16[2,3,256]{2,0,1:T(2,128)(2,1)}, bf16[2,3,256]{2,0,1:T(2,128)(2,1)S(1)}, u32[]{:S(2)}, u32[]{:S(2)}) %collective-permute-start) | collective-permute-done | bytes 3104 | tf_op jit(solution)/shard_map/ppermute | solution.py:15
  119.9 6.4 %all-to-all-start = ((f32[3,256,128]{2,0,1:T(4,128)}), f32[3,256,128]{2,0,1:T(4,128)}, u32[]{:S(2)}, u32[]{:S(2)}) async-start(f32[3,256,128]{2,0,1:T(4,128)} %copy.87), calls=%async_computation | async-start | bytes 1048576 | tf_op jit(solution)/shard_map/all_to_all | solution.py:53
  131.4 11.4 %all-to-all-done = f32[3,256,128]{2,0,1:T(4,128)} async-done(((f32[3,256,128]{2,0,1:T(4,128)}), f32[3,256,128]{2,0,1:T(4,128)}, u32[]{:S(2)}, u32[]{:S(2)}) %all-to-all-start) | async-done | bytes 393248 | tf_op jit(solution)/shard_map/all_to_all | solution.py:53
  142.9 2.6 convolution_bitcast_fusion.1
  161.9 20.8 %all_to_all.20 = f32[64,3,4,128]{3,2,1,0:T(4,128)S(1)} all-to-all(f32[64,3,4,128]{3,2,1,0:T(4,128)S(1)} %copy.102), channel_id=1, replica_groups=mesh['seq'=64,'ch'=4] {'seq'}, dimensions={0} | all-to-all | bytes 786432 | tf_op jit(solution)/shard_map/all_to_all | solution.py:61
  187.9 2.9 collective-permute-start.9
  192.2 5.9 %fusion.155 = (bf16[128,4096]{1,0:T(8,128)(2,1)}, f32[128]{0:T(128)S(1)}) fusion(bf16[128,4096]{1,0:T(8,128)(2,1)S(1)} %copy-done, f32[4096]{0:T(1024)S(1)} %copy-done.11, bf16[4096,3,256]{2,0,1:T(8,128)(2,1)} %all-gather.3.cloned.1.call-done, f32[130,3,256]{2,0,1:T(8,128)S(1)} %pad_maximum_fusion.11, f32[3,256]{1,0:T(4,128)S(1)} %get-tuple-element.38, ...), kind=kOutput, calls=%fused_computation.228 | convolution fusion | flops 808714112 | bytes 9597440 | tf_op jit(solution)/shard_map/dot_general | solution.py:182
  199.6 2.6 reshape.677
  203.1 2.8 pad_maximum_fusion
  205.9 3.4 %copy.129 = bf16[128,4,1152]{0,2,1:T(8,128)(2,1)} copy(bf16[128,4,1152]{2,1,0:T(4,128)(2,1)} %pad_maximum_fusion) | data formatting | bytes 2359296
  211.1 3.1 %fusion = f32[128,4096]{1,0:T(8,128)} fusion(bf16[4096,256]{1,0:T(8,128)(2,1)S(1)} %bitcast.172, f32[128,1,256]{2,0,1:T(8,128)} %copy.103, f32[128,3,256]{2,0,1:T(8,128)S(1)} %fusion.24, f32[256]{0:T(256)S(1)} %copy-done.9), kind=kOutput, calls=%fused_computation.2 | convolution fusion | flops 269647872 | bytes 4719616 | tf_op jit(solution)/shard_map/dot_general | solution.py:166
  214.2 3.0 %reshape.679 = f32[128,2,2,1024]{3,2,1,0:T(2,128)S(1)} reshape(f32[128,4096]{1,0:T(8,128)} %fusion) | data formatting | bytes 4194304 | tf_op jit(solution)/shard_map/convert_element_type | solution.py:41
  218.6 3.0 %collective-permute-start.7 = (bf16[128,2,1024]{2,0,1:T(8,128)(2,1)}, bf16[128,2,1024]{2,0,1:T(8,128)(2,1)}, u32[]{:S(2)}, u32[]{:S(2)}) collective-permute-start(bf16[128,2,1024]{2,0,1:T(8,128)(2,1)} %bitcast.169), channel_id=1, source_target_pairs={{0,2},{1,3},{2,0},{3,1},{4,6},{5,7},{6,4},{7,5},{8,10},{9,11},{10,... | collective-permute-start | bytes 1572872 | tf_op jit(solution)/shard_map/ppermute | solution.py:47
  221.7 21.9 %collective-permute-done.7 = bf16[128,2,1024]{2,0,1:T(8,128)(2,1)} collective-permute-done((bf16[128,2,1024]{2,0,1:T(8,128)(2,1)}, bf16[128,2,1024]{2,0,1:T(8,128)(2,1)}, u32[]{:S(2)}, u32[]{:S(2)}) %collective-permute-start.7) | collective-permute-done | bytes 524320 | tf_op jit(solution)/shard_map/ppermute | solution.py:47
  249.0 5.7 %collective-permute-done.8 = bf16[128,1024]{1,0:T(8,128)(2,1)} collective-permute-done((bf16[128,1024]{1,0:T(8,128)(2,1)}, bf16[128,1024]{1,0:T(8,128)(2,1)}, u32[]{:S(2)}, u32[]{:S(2)}) %collective-permute-start.8) | collective-permute-done | bytes 262176 | tf_op jit(solution)/shard_map/ppermute | solution.py:47
  257.8 23.2 %all-gather.5.cloned.1.call-done = bf16[128,4096]{1,0:T(8,128)(2,1)} async-done(((bf16[128,1024]{1,0:T(8,128)(2,1)}), bf16[128,4096]{1,0:T(8,128)(2,1)}) %all-gather.5.cloned.1.call-update) | async-done | bytes 1048592 | tf_op jit(solution)/shard_map/all_gather | solution.py:209
  (128 shorter events, 65.8 us)
Async XLA Ops:
  7.2 88.0 %all-gather.3.cloned.1.call-start = ((), (), s32[]{:S(2)}) async-start(), calls=%async_computation.3 | async-start | bytes 6389760 | tf_op jit(solution)/shard_map/all_gather | solution.py:129
  7.9 5.7 %collective-permute-start.1 = (bf16[64,256]{1,0:T(8,128)(2,1)}, bf16[64,256]{1,0:T(8,128)(2,1)S(1)}, u32[]{:S(2)}, u32[]{:S(2)}) collective-permute-start(bf16[64,256]{1,0:T(8,128)(2,1)} %bitcast.192), channel_id=1, source_target_pairs={{0,128},{4,132},{8,136},{12,140},{16,144},{20,148},{24,152},{28,15... | collective-permute-start | bytes 98312 | tf_op jit(solution)/shard_map/ppermute | solution.py:26
  14.5 4.6 %collective-permute-start.2 = (bf16[2,64,256]{2,1,0:T(8,128)(2,1)S(1)}, bf16[2,64,256]{2,1,0:T(8,128)(2,1)S(1)}, u32[]{:S(2)}, u32[]{:S(2)}) collective-permute-start(bf16[2,64,256]{2,1,0:T(8,128)(2,1)S(1)} %maximum_select_fusion.5), channel_id=1, source_target_pairs={{0,64},{4,68},{8,72},{12,76},{16,80},{20,84},{24,88},{28,92},{32,9... | collective-permute-start | bytes 196616 | tf_op jit(solution)/shard_map/ppermute | solution.py:26
  19.0 26.6 %copy-start.8 = (f32[3,3,256]{2,1,0:T(4,128)S(1)}, f32[3,3,256]{2,1,0:T(4,128)}, u32[]{:S(2)}) copy-start(f32[3,3,256]{2,1,0:T(4,128)} %param.11) | copy-start | bytes 27652
  19.1 11.5 %collective-permute-start.3 = (bf16[2,2,64,256]{3,2,0,1:T(8,128)(2,1)S(1)}, bf16[2,2,64,256]{3,2,0,1:T(8,128)(2,1)S(1)}, u32[]{:S(2)}, u32[]{:S(2)}) collective-permute-start(bf16[2,2,64,256]{3,2,0,1:T(8,128)(2,1)S(1)} %maximum_select_fusion.4), channel_id=1, source_target_pairs={{0,32},{4,36},{8,40},{12,44},{16,48},{20,52},{24,56},{28,60},{32,0... | collective-permute-start | bytes 393224 | tf_op jit(solution)/shard_map/ppermute | solution.py:26
  30.6 14.2 %collective-permute-start.4 = (bf16[2,2,2,64,256]{4,3,0,1,2:T(8,128)(2,1)S(1)}, bf16[2,2,2,64,256]{4,3,0,1,2:T(8,128)(2,1)S(1)}, u32[]{:S(2)}, u32[]{:S(2)}) collective-permute-start(bf16[2,2,2,64,256]{4,3,0,1,2:T(8,128)(2,1)S(1)} %maximum_select_fusion.3), channel_id=1, source_target_pairs={{0,16},{4,20},{8,24},{12,28},{16,0},{20,4},{24,8},{28,12},{32,48},... | collective-permute-start | bytes 786440 | tf_op jit(solution)/shard_map/ppermute | solution.py:26
  45.7 14.5 %collective-permute-start.5 = (bf16[2,2,2,2,64,256]{5,4,0,1,2,3:T(8,128)(2,1)}, bf16[2,2,2,2,64,256]{5,4,0,1,2,3:T(8,128)(2,1)S(1)}, u32[]{:S(2)}, u32[]{:S(2)}) collective-permute-start(bf16[2,2,2,2,64,256]{5,4,0,1,2,3:T(8,128)(2,1)} %maximum_select_fusion.2), channel_id=1, source_target_pairs={{0,8},{4,12},{8,0},{12,4},{16,24},{20,28},{24,16},{28,20},{32,40},... | collective-permute-start | bytes 1572872 | tf_op jit(solution)/shard_map/ppermute | solution.py:26
  45.8 14.6 %copy-start = (bf16[128,4096]{1,0:T(8,128)(2,1)S(1)}, bf16[128,4096]{1,0:T(8,128)(2,1)}, u32[]{:S(2)}) copy-start(bf16[128,4096]{1,0:T(8,128)(2,1)} %param.8) | copy-start | bytes 3145732
  60.3 2.7 collective-permute-start.6
  61.3 42.6 %copy-start.13 = (f32[128]{0:T(128)}, f32[128]{0:T(128)S(1)}, u32[]{:S(2)}) copy-start(f32[128]{0:T(128)S(1)} %get-tuple-element.37) | copy-start | bytes 1540
  63.2 40.7 %copy-start.10 = (f32[4096]{0:T(1024)S(1)}, f32[4096]{0:T(1024)}, u32[]{:S(2)}) copy-start(f32[4096]{0:T(1024)} %param.9) | copy-start | bytes 49156
  103.9 7.8 %copy-start.4 = (bf16[128,4096]{1,0:T(8,128)(2,1)S(1)}, bf16[128,4096]{1,0:T(8,128)(2,1)}, u32[]{:S(2)}) copy-start(bf16[128,4096]{1,0:T(8,128)(2,1)} %param.15) | copy-start | bytes 3145732
  109.6 7.2 %collective-permute-start = (bf16[2,3,256]{2,0,1:T(2,128)(2,1)}, bf16[2,3,256]{2,0,1:T(2,128)(2,1)S(1)}, u32[]{:S(2)}, u32[]{:S(2)}) collective-permute-start(bf16[2,3,256]{2,0,1:T(2,128)(2,1)} %bitcast.1), channel_id=1, source_target_pairs={{0,4},{4,8},{8,12},{12,16},{16,20},{20,24},{24,28},{28,32},{32,36}... | collective-permute-start | bytes 9224 | tf_op jit(solution)/shard_map/ppermute | solution.py:15
  119.9 23.0 %all-to-all-start = ((f32[3,256,128]{2,0,1:T(4,128)}), f32[3,256,128]{2,0,1:T(4,128)}, u32[]{:S(2)}, u32[]{:S(2)}) async-start(f32[3,256,128]{2,0,1:T(4,128)} %copy.87), calls=%async_computation | async-start | bytes 1048576 | tf_op jit(solution)/shard_map/all_to_all | solution.py:53
  126.3 121.3 %reduce-scatter.4.cloned.1.call-start = ((), (), s32[]{:S(2)}) async-start(), calls=%async_computation.5 | async-start | bytes 1474560
  160.5 26.3 %copy-start.9 = (f32[256]{0:T(256)S(1)}, f32[256]{0:T(256)}, u32[]{:S(2)}) copy-start(f32[256]{0:T(256)} %param.13) | copy-start | bytes 3076
  186.7 5.4 %copy-start.11 = (f32[4096]{0:T(1024)S(1)}, f32[4096]{0:T(1024)}, u32[]{:S(2)}) copy-start(f32[4096]{0:T(1024)} %param.9) | copy-start | bytes 49156
  187.9 4.2 %collective-permute-start.9 = (f32[2,3,256]{2,0,1:T(2,128)S(1)}, f32[2,3,256]{2,0,1:T(2,128)S(1)}, u32[]{:S(2)}, u32[]{:S(2)}) collective-permute-start(f32[2,3,256]{2,0,1:T(2,128)S(1)} %slice.125), channel_id=1, source_target_pairs={{4,0},{8,4},{12,8},{16,12},{20,16},{24,20},{28,24},{32,28},{36,32}... | collective-permute-start | bytes 18440 | tf_op jit(solution)/shard_map/ppermute | solution.py:15
  209.4 71.7 %all-gather.5.cloned.1.call-start = ((), (), s32[]{:S(2)}) async-start(), calls=%async_computation.4 | async-start | bytes 1310720 | tf_op jit(solution)/shard_map/all_gather | solution.py:209
  218.6 25.0 %collective-permute-start.7 = (bf16[128,2,1024]{2,0,1:T(8,128)(2,1)}, bf16[128,2,1024]{2,0,1:T(8,128)(2,1)}, u32[]{:S(2)}, u32[]{:S(2)}) collective-permute-start(bf16[128,2,1024]{2,0,1:T(8,128)(2,1)} %bitcast.169), channel_id=1, source_target_pairs={{0,2},{1,3},{2,0},{3,1},{4,6},{5,7},{6,4},{7,5},{8,10},{9,11},{10,... | collective-permute-start | bytes 1572872 | tf_op jit(solution)/shard_map/ppermute | solution.py:47
  246.1 8.6 %copy-start.12 = (f32[128]{0:T(128)S(1)}, f32[128]{0:T(128)}, u32[]{:S(2)}) copy-start(f32[128]{0:T(128)} %get-tuple-element.36) | copy-start | bytes 1540
  246.1 8.6 %copy-start.14 = (f32[128]{0:T(128)S(1)}, f32[128]{0:T(128)}, u32[]{:S(2)}) copy-start(f32[128]{0:T(128)} %copy-done.13) | copy-start | bytes 1540
  246.1 8.6 %collective-permute-start.8 = (bf16[128,1024]{1,0:T(8,128)(2,1)}, bf16[128,1024]{1,0:T(8,128)(2,1)}, u32[]{:S(2)}, u32[]{:S(2)}) collective-permute-start(bf16[128,1024]{1,0:T(8,128)(2,1)} %fusion.34), channel_id=1, source_target_pairs={{0,1},{1,0},{2,3},{3,2},{4,5},{5,4},{6,7},{7,6},{8,9},{9,8},{10,11... | collective-permute-start | bytes 786440 | tf_op jit(solution)/shard_map/ppermute | solution.py:47
  248.8 8.2 %copy-start.6 = (f32[1,128,64,4]{1,3,0,2:T(4,128)S(1)}, f32[1,128,64,4]{1,3,0,2:T(4,128)}, u32[]{:S(2)}) copy-start(f32[1,128,64,4]{1,3,0,2:T(4,128)} %get-tuple-element.26) | copy-start | bytes 393220
  (6 other events, 23.1 us)
Sparse Core Ops, SparseCore 0:
  10.8 84.3 all-gather.2
  209.5 31.8 reduce-scatter.3
  257.1 23.8 all-gather.4
